TPU v7x, 1024 devices: a whole 4x4x32 slice. The times are simulated.
1024 devices in a mesh: gx: 64 (over z, core), gy: 16 (over y, x).
Axes of the slice: x: 4, y: 4, z: 32, core: 2. Of those that a mesh axis runs over, the one named last changes fastest.
Arguments:
- source: float32 [512, 256, 128], P('gx', 'gy'), may hold values from -6 to 6, as said below
- coupling_x: float32 [512, 256, 128], P('gx', 'gy'), may hold values from 128 to 512
- coupling_y: float32 [512, 256, 128], P('gx', 'gy'), may hold values from 128 to 512
- reaction: float32 [512, 256, 128], P('gx', 'gy'), may hold values from 0.03 to 0.12
Outputs:
- advanced: float32 [512, 256, 128], P('gx', 'gy')
Inputs may be any that keep to these rules, and one draw needn't show every extreme that they name: source terms of the sub-step.
All inputs are finite; a program needn't handle non-finite values.
Results may differ from a plain program's by a relative error of at most 0.002.
Values sent between devices are 32-bit elements; how exact they have to be, the bound alone decides.
No kernel may reach another device: no remote copies, remote signals or barrier semaphores. Data moves between devices by JAX's collectives and lax.ppermute only.
A program may use at most 64 MiB of HBM per device.

v0:
```python
from functools import reduce

import jax
import jax.numpy as jnp
from jax import lax
from jax.sharding import PartitionSpec as P


def entering_2(x, axis, combine, identity, reverse):
    count, here = (lax.axis_size(axis), lax.axis_index(axis))
    everything = jax.tree.map(lambda part: lax.all_gather(part, axis), x)
    start = jax.tree.map(
        lambda part, zero: jnp.broadcast_to(jnp.asarray(zero, part.dtype), part.shape), x, identity
    )

    def turn(k, before):
        at = count - 1 - k if reverse else k
        reached = at > here if reverse else at < here
        new = combine(before, jax.tree.map(lambda part: part[at], everything))
        return jax.tree.map(lambda a, b: jnp.where(reached, a, b), new, before)

    return lax.fori_loop(0, count, turn, start)


def compose(left, right):
    entries = []
    for row_idx in range(3):
        for col_idx in range(3):
            entries.append(
                reduce(
                    lambda acc, term: acc + term,
                    [
                        left[3 * row_idx + mid_idx] * right[3 * mid_idx + col_idx]
                        for mid_idx in range(3)
                    ],
                )
            )
    largest = reduce(jnp.maximum, [jnp.abs(entry) for entry in entries])
    return tuple((entry / largest for entry in entries))


def chain_matrices(earlier, later):
    return compose(later, earlier)


def linked_transforms(earlier, later):
    return (later[0] + later[1] * earlier[0], later[1] * earlier[1])


def unit_matrix(sample):
    zero_field = jnp.zeros_like(sample)
    one_field = jnp.ones_like(sample)
    return (
        one_field,
        zero_field,
        zero_field,
        zero_field,
        one_field,
        zero_field,
        zero_field,
        zero_field,
        one_field,
    )


def cell_matrices(source, neighbor_coupling, reaction):
    zero_field = jnp.zeros_like(source)
    return (
        zero_field,
        zero_field,
        -neighbor_coupling,
        zero_field,
        neighbor_coupling,
        source,
        neighbor_coupling,
        zero_field,
        reaction + 2.0 * neighbor_coupling,
    )


def solve_lines(source, neighbor_coupling, reaction, solve_direction, enter_fn, leave_fn):
    prefix = lax.associative_scan(
        lambda earlier, later: compose(later, earlier),
        cell_matrices(source, neighbor_coupling, reaction),
        axis=solve_direction,
    )
    totals = tuple(
        (
            lax.index_in_dim(
                entry, entry.shape[solve_direction] - 1, solve_direction, keepdims=False
            )
            for entry in prefix
        )
    )
    entering = enter_fn(totals)
    state_x = jnp.expand_dims(entering[2], solve_direction)
    state_y = jnp.expand_dims(entering[5], solve_direction)
    state_z = jnp.expand_dims(entering[8], solve_direction)
    updated_streamwise = prefix[0] * state_x + prefix[1] * state_y + prefix[2] * state_z
    new_y = prefix[3] * state_x + prefix[4] * state_y + prefix[5] * state_z
    updated_normal = prefix[6] * state_x + prefix[7] * state_y + prefix[8] * state_z
    eliminate_factor = updated_streamwise / updated_normal
    offset_values = new_y / updated_normal

    def combine_transforms(later, current):
        return (current[0] + current[1] * later[0], current[1] * later[1])

    back_maps = lax.associative_scan(
        combine_transforms, (offset_values, -eliminate_factor), reverse=True, axis=solve_direction
    )
    first_maps = tuple(
        (lax.index_in_dim(entry, 0, solve_direction, keepdims=False) for entry in back_maps)
    )
    beyond = leave_fn(first_maps)
    return back_maps[0] + back_maps[1] * jnp.expand_dims(beyond, solve_direction)


def per_device(source, coupling_x, coupling_y, reaction):

    def x_enter(totals):
        return entering_2(totals, "gx", chain_matrices, unit_matrix(totals[0]), False)

    def x_leave(first_maps):
        return entering_2(
            first_maps,
            "gx",
            linked_transforms,
            (jnp.zeros_like(first_maps[0]), jnp.ones_like(first_maps[0])),
            True,
        )[0]

    halfway = solve_lines(source, coupling_x, reaction, 0, x_enter, x_leave)

    def y_enter(totals):
        return entering_2(totals, "gy", chain_matrices, unit_matrix(totals[0]), False)

    def y_leave(first_maps):
        return entering_2(
            first_maps,
            "gy",
            linked_transforms,
            (jnp.zeros_like(first_maps[0]), jnp.ones_like(first_maps[0])),
            True,
        )[0]

    advanced = solve_lines(halfway, coupling_y, reaction, 1, y_enter, y_leave)
    return advanced


def solution(mesh):
    placed = (P("gx", "gy", None), P("gx", "gy", None), P("gx", "gy", None), P("gx", "gy", None))
    return jax.shard_map(
        per_device, mesh=mesh, in_specs=placed, out_specs=P("gx", "gy", None), check_vma=False
    )
```

profile of v0, /device:TPU:2, one launch (start us, length us, event | category | flops | bytes accessed | tf_op | source)
XLA Modules:
  0.0 1001.0 jit_solution(5555402527207044744)
XLA Ops:
  0.0 1.0 copy_negate_fusion.1
  9.2 70.2 %all_gather.73 = f32[64,16,128]{2,1,0:T(8,128)S(1)} all-gather(f32[1,16,128]{2,1,0:T(8,128)S(1)} %bitcast.495), channel_id=1, replica_groups=mesh['gx'=64,'gy'=16] {'gx'}, dimensions={0}, use_global_device_ids=true | all-gather | bytes 532480 | tf_op jit(solution)/shard_map/all_gather | solution.py:11
  80.8 53.8 %all_gather.74 = f32[64,16,128]{2,1,0:T(8,128)S(1)} all-gather(f32[1,16,128]{2,1,0:T(8,128)S(1)} %bitcast.496), channel_id=1, replica_groups=mesh['gx'=64,'gy'=16] {'gx'}, dimensions={0}, use_global_device_ids=true | all-gather | bytes 532480 | tf_op jit(solution)/shard_map/all_gather | solution.py:11
  136.7 55.1 %all_gather.72 = f32[64,16,128]{2,1,0:T(8,128)S(1)} all-gather(f32[1,16,128]{2,1,0:T(8,128)S(1)} %bitcast.497), channel_id=1, replica_groups=mesh['gx'=64,'gy'=16] {'gx'}, dimensions={0}, use_global_device_ids=true | all-gather | bytes 532480 | tf_op jit(solution)/shard_map/all_gather | solution.py:11
  193.4 53.8 %all_gather.71 = f32[64,16,128]{2,1,0:T(8,128)S(1)} all-gather(f32[1,16,128]{2,1,0:T(8,128)S(1)} %bitcast.498), channel_id=1, replica_groups=mesh['gx'=64,'gy'=16] {'gx'}, dimensions={0}, use_global_device_ids=true | all-gather | bytes 532480 | tf_op jit(solution)/shard_map/all_gather | solution.py:11
  248.5 55.1 %all_gather.70 = f32[64,16,128]{2,1,0:T(8,128)S(1)} all-gather(f32[1,16,128]{2,1,0:T(8,128)S(1)} %bitcast.499), channel_id=1, replica_groups=mesh['gx'=64,'gy'=16] {'gx'}, dimensions={0}, use_global_device_ids=true | all-gather | bytes 532480 | tf_op jit(solution)/shard_map/all_gather | solution.py:11
  305.0 53.8 %all_gather.69 = f32[64,16,128]{2,1,0:T(8,128)S(1)} all-gather(f32[1,16,128]{2,1,0:T(8,128)S(1)} %bitcast.500), channel_id=1, replica_groups=mesh['gx'=64,'gy'=16] {'gx'}, dimensions={0}, use_global_device_ids=true | all-gather | bytes 532480 | tf_op jit(solution)/shard_map/all_gather | solution.py:11
  359.4 5.5 pad.535
  364.8 1.4 pad_maximum_fusion.4
  366.3 5.5 pad.534
  371.8 60.3 %all_gather.68 = f32[64,16,128]{2,1,0:T(8,128)} all-gather(f32[1,16,128]{2,1,0:T(8,128)S(1)} %bitcast.501), channel_id=1, replica_groups=mesh['gx'=64,'gy'=16] {'gx'}, dimensions={0}, use_global_device_ids=true | all-gather | bytes 532480 | tf_op jit(solution)/shard_map/all_gather | solution.py:11
  432.7 5.5 pad.533
  438.8 5.5 pad.532
  444.3 59.0 %all_gather.67 = f32[64,16,128]{2,1,0:T(8,128)} all-gather(f32[1,16,128]{2,1,0:T(8,128)S(1)} %bitcast.502), channel_id=1, replica_groups=mesh['gx'=64,'gy'=16] {'gx'}, dimensions={0}, use_global_device_ids=true | all-gather | bytes 532480 | tf_op jit(solution)/shard_map/all_gather | solution.py:11
  504.0 5.5 pad.531
  510.0 5.5 pad.530
  515.5 60.3 %all_gather.66 = f32[64,16,128]{2,1,0:T(8,128)} all-gather(f32[1,16,128]{2,1,0:T(8,128)S(1)} %bitcast.503), channel_id=1, replica_groups=mesh['gx'=64,'gy'=16] {'gx'}, dimensions={0}, use_global_device_ids=true | all-gather | bytes 532480 | tf_op jit(solution)/shard_map/all_gather | solution.py:11
  575.9 54.3 %while.92 = (s32[]{:T(128)}, f32[16,128]{1,0:T(8,128)S(1)}, f32[16,128]{1,0:T(8,128)S(1)}, f32[16,128]{1,0:T(8,128)S(1)}, f32[16,128]{1,0:T(8,128)S(1)}, /*index...) while((s32[]{:T(128)}, f32[16,128]{1,0:T(8,128)S(1)}, ...), condition=%wide.region_1.2_spmd.clone, body=%wide.region_0.1_spmd.clone.sunk | while | flops 198660 | bytes 434399 | solution.py:22
  577.6 0.8 divide_select_fusion.22
  578.5 0.8 divide_select_fusion.22
  579.3 0.8 divide_select_fusion.22
  580.2 0.8 divide_select_fusion.22
  581.0 0.8 divide_select_fusion.22
  581.9 0.8 divide_select_fusion.22
  582.7 0.8 divide_select_fusion.22
  583.6 0.8 divide_select_fusion.22
  584.4 0.8 divide_select_fusion.22
  585.2 0.8 divide_select_fusion.22
  586.1 0.8 divide_select_fusion.22
  586.9 0.8 divide_select_fusion.22
  587.8 0.8 divide_select_fusion.22
  588.6 0.8 divide_select_fusion.22
  630.3 1.3 divide_negate_fusion.1
  633.7 54.0 %all_gather.76 = f32[64,16,128]{2,1,0:T(8,128)S(1)} all-gather(f32[1,16,128]{2,1,0:T(8,128)S(1)} %bitcast.504), channel_id=1, replica_groups=mesh['gx'=64,'gy'=16] {'gx'}, dimensions={0}, use_global_device_ids=true | all-gather | bytes 532480 | tf_op jit(solution)/shard_map/all_gather | solution.py:11
  688.0 55.1 %all_gather.75 = f32[64,16,128]{2,1,0:T(8,128)S(1)} all-gather(f32[1,16,128]{2,1,0:T(8,128)S(1)} %bitcast.505), channel_id=1, replica_groups=mesh['gx'=64,'gy'=16] {'gx'}, dimensions={0}, use_global_device_ids=true | all-gather | bytes 532480 | tf_op jit(solution)/shard_map/all_gather | solution.py:11
  743.2 2.9 while.93
  748.8 23.7 %all-gather.8 = f32[128,1,128]{2,1,0:T(1,128)S(1)} all-gather(f32[8,1,128]{2,1,0:T(1,128)S(1)} %bitcast.532), channel_id=10, replica_groups=mesh['gx'=64,'gy'=16] {'gy'}, dimensions={0}, use_global_device_ids=true | all-gather | bytes 69632 | tf_op jit(solution)/shard_map/all_gather | solution.py:11
  772.7 21.5 %all-gather.7 = f32[128,1,128]{2,1,0:T(1,128)S(1)} all-gather(f32[8,1,128]{2,1,0:T(1,128)S(1)} %bitcast.533), channel_id=9, replica_groups=mesh['gx'=64,'gy'=16] {'gy'}, dimensions={0}, use_global_device_ids=true | all-gather | bytes 69632 | tf_op jit(solution)/shard_map/all_gather | solution.py:11
  794.3 23.1 %all-gather.6 = f32[128,1,128]{2,1,0:T(1,128)S(1)} all-gather(f32[8,1,128]{2,1,0:T(1,128)S(1)} %bitcast.534), channel_id=8, replica_groups=mesh['gx'=64,'gy'=16] {'gy'}, dimensions={0}, use_global_device_ids=true | all-gather | bytes 69632 | tf_op jit(solution)/shard_map/all_gather | solution.py:11
  817.6 21.4 %all-gather.5 = f32[128,1,128]{2,1,0:T(1,128)S(1)} all-gather(f32[8,1,128]{2,1,0:T(1,128)S(1)} %bitcast.535), channel_id=7, replica_groups=mesh['gx'=64,'gy'=16] {'gy'}, dimensions={0}, use_global_device_ids=true | all-gather | bytes 69632 | tf_op jit(solution)/shard_map/all_gather | solution.py:11
  839.2 23.1 %all-gather.4 = f32[128,1,128]{2,1,0:T(1,128)S(1)} all-gather(f32[8,1,128]{2,1,0:T(1,128)S(1)} %bitcast.536), channel_id=6, replica_groups=mesh['gx'=64,'gy'=16] {'gy'}, dimensions={0}, use_global_device_ids=true | all-gather | bytes 69632 | tf_op jit(solution)/shard_map/all_gather | solution.py:11
  862.5 21.5 %all-gather.3 = f32[128,1,128]{2,1,0:T(1,128)S(1)} all-gather(f32[8,1,128]{2,1,0:T(1,128)S(1)} %bitcast.537), channel_id=5, replica_groups=mesh['gx'=64,'gy'=16] {'gy'}, dimensions={0}, use_global_device_ids=true | all-gather | bytes 69632 | tf_op jit(solution)/shard_map/all_gather | solution.py:11
  884.2 23.1 %all-gather.2 = f32[128,1,128]{2,1,0:T(1,128)S(1)} all-gather(f32[8,1,128]{2,1,0:T(1,128)S(1)} %bitcast.538), channel_id=4, replica_groups=mesh['gx'=64,'gy'=16] {'gy'}, dimensions={0}, use_global_device_ids=true | all-gather | bytes 69632 | tf_op jit(solution)/shard_map/all_gather | solution.py:11
  907.4 21.5 %all-gather.1 = f32[128,1,128]{2,1,0:T(1,128)S(1)} all-gather(f32[8,1,128]{2,1,0:T(1,128)S(1)} %bitcast.539), channel_id=3, replica_groups=mesh['gx'=64,'gy'=16] {'gy'}, dimensions={0}, use_global_device_ids=true | all-gather | bytes 69632 | tf_op jit(solution)/shard_map/all_gather | solution.py:11
  929.1 23.1 %all-gather = f32[128,1,128]{2,1,0:T(1,128)S(1)} all-gather(f32[8,1,128]{2,1,0:T(1,128)S(1)} %bitcast.540), channel_id=2, replica_groups=mesh['gx'=64,'gy'=16] {'gy'}, dimensions={0}, use_global_device_ids=true | all-gather | bytes 69632 | tf_op jit(solution)/shard_map/all_gather | solution.py:11
  952.2 1.7 while.94
  954.8 21.5 %all-gather.10 = f32[128,1,128]{2,1,0:T(1,128)S(1)} all-gather(f32[8,1,128]{2,1,0:T(1,128)S(1)} %bitcast.541), channel_id=12, replica_groups=mesh['gx'=64,'gy'=16] {'gy'}, dimensions={0}, use_global_device_ids=true | all-gather | bytes 69632 | tf_op jit(solution)/shard_map/all_gather | solution.py:11
  976.5 23.1 %all-gather.9 = f32[128,1,128]{2,1,0:T(1,128)S(1)} all-gather(f32[8,1,128]{2,1,0:T(1,128)S(1)} %bitcast.542), channel_id=11, replica_groups=mesh['gx'=64,'gy'=16] {'gy'}, dimensions={0}, use_global_device_ids=true | all-gather | bytes 69632 | tf_op jit(solution)/shard_map/all_gather | solution.py:11
  (696 shorter events, 69.3 us)
Async XLA Ops:
  1.0 0.8 copy-start
  1.1 0.9 copy-start.32
  4.4 3.8 copy-start.24
  4.6 3.5 copy-start.26
  5.4 2.8 copy-start.28
  5.6 2.6 copy-start.30
  9.2 70.3 %copy-start.1 = (f32[8,16,128]{2,0,1:T(8,128)}, f32[8,16,128]{2,0,1:T(8,128)S(1)}, u32[]{:S(2)}) copy-start(f32[8,16,128]{2,0,1:T(8,128)S(1)} %pad.542) | copy-start | bytes 196612
  79.6 0.6 copy-start.2
  80.2 0.6 copy-start.3
  134.6 0.7 slice-start
  135.4 0.6 copy-start.4
  136.0 0.6 copy-start.5
  191.9 0.9 copy-start.12
  191.9 0.7 slice-start.1
  192.8 0.6 copy-start.14
  247.3 0.6 copy-start.16
  247.9 0.6 copy-start.18
  303.7 0.6 copy-start.20
  304.4 0.6 copy-start.22
  364.8 6.9 copy-start.6
  371.7 60.4 %copy-start.7 = (f32[8,16,128]{2,0,1:T(8,128)}, f32[8,16,128]{2,0,1:T(8,128)S(1)}, u32[]{:S(2)}) copy-start(f32[8,16,128]{2,0,1:T(8,128)S(1)} %pad.534) | copy-start | bytes 196612
  371.7 60.3 %copy-start.25 = (f32[4,16,128]{2,0,1:T(4,128)S(1)}, f32[4,16,128]{2,0,1:T(4,128)}, u32[]{:S(2)}) copy-start(f32[4,16,128]{2,0,1:T(4,128)} %copy-done.24) | copy-start | bytes 98308
  371.8 60.3 %copy-start.27 = (f32[4,16,128]{2,0,1:T(4,128)S(1)}, f32[4,16,128]{2,0,1:T(4,128)}, u32[]{:S(2)}) copy-start(f32[4,16,128]{2,0,1:T(4,128)} %copy-done.26) | copy-start | bytes 98308
  432.7 5.5 copy-start.34
  438.2 6.1 copy-start.8
  444.3 59.0 %copy-start.9 = (f32[8,16,128]{2,0,1:T(8,128)}, f32[8,16,128]{2,0,1:T(8,128)S(1)}, u32[]{:S(2)}) copy-start(f32[8,16,128]{2,0,1:T(8,128)S(1)} %pad.532) | copy-start | bytes 196612
  444.3 59.0 %copy-start.29 = (f32[4,16,128]{2,0,1:T(4,128)S(1)}, f32[4,16,128]{2,0,1:T(4,128)}, u32[]{:S(2)}) copy-start(f32[4,16,128]{2,0,1:T(4,128)} %copy-done.28) | copy-start | bytes 98308
  444.3 59.0 %copy-start.31 = (f32[4,16,128]{2,0,1:T(4,128)S(1)}, f32[4,16,128]{2,0,1:T(4,128)}, u32[]{:S(2)}) copy-start(f32[4,16,128]{2,0,1:T(4,128)} %copy-done.30) | copy-start | bytes 98308
  503.9 5.5 copy-start.33
  509.4 6.1 copy-start.10
  515.5 60.3 %copy-start.11 = (f32[8,16,128]{2,0,1:T(8,128)}, f32[8,16,128]{2,0,1:T(8,128)S(1)}, u32[]{:S(2)}) copy-start(f32[8,16,128]{2,0,1:T(8,128)S(1)} %pad.530) | copy-start | bytes 196612
  630.2 1.3 copy-start.13
  630.2 1.3 copy-start.15
  630.2 1.3 copy-start.17
  630.2 1.3 copy-start.19
  630.2 1.3 copy-start.21
  630.3 1.3 copy-start.23
where the time goes:
time: 1010 us; the launch traced here: 1000 us
  blocking collectives  877 us (87%)
  other arithmetic  63.5 us (6%)
  local copies, waits for them, and re-layouts  52.7 us (5%)
    all_gather x22, blocking collectives, entering_2(): everything = jax.tree.map(lambda part: lax.all_gather(part, axis), x)  877 us
    select_n x240, other arithmetic, turn(): return jax.tree.map(lambda a, b: jnp.where(reached, a, b), new, before)  54.2 us
    pad x90, local copies, waits for them, and re-layouts, solve_lines(): lax.associative_scan(lambda earlier, later: compose(later, earlier), cell...  40.2 us

commit v1 on v0

v1 whole, which is shorter than its diff:
```python
import jax
import jax.numpy as jnp
from jax import lax
from jax.experimental import pallas as pl
from jax.sharding import PartitionSpec as P


def local_kernel(f_ref, k_ref, r_ref, a_ref, b_ref, c_ref):
    n = f_ref.shape[0]
    zero = jnp.zeros(f_ref.shape[1:], f_ref.dtype)
    ratio, shifted, shifted_b = zero, zero, zero
    for i in range(n):
        link = k_ref[i]
        denom = r_ref[i] + 2.0 * link + link * ratio
        ratio = -link / denom
        shifted = (f_ref[i] + link * shifted) / denom
        shifted_b = (link if i == 0 else link * shifted_b) / denom
        a_ref[i] = shifted
        b_ref[i] = shifted_b
        c_ref[i] = ratio
    later_a = a_ref[n - 1]
    later_b = b_ref[n - 1]
    later_c = k_ref[n - 1] / denom
    c_ref[n - 1] = later_c
    for i in range(n - 2, -1, -1):
        ratio = c_ref[i]
        later_a = a_ref[i] - ratio * later_a
        later_b = b_ref[i] - ratio * later_b
        later_c = -ratio * later_c
        a_ref[i] = later_a
        b_ref[i] = later_b
        c_ref[i] = later_c


def local_solve(f, k, r):
    shape = jax.ShapeDtypeStruct(f.shape, f.dtype)
    return pl.pallas_call(local_kernel, out_shape=(shape, shape, shape))(f, k, r)


def reduced_kernel(coef_ref, out_ref):
    count = coef_ref.shape[0]
    gains = []
    p_prev = None
    q_prev = None
    for d in range(count):
        row = coef_ref[d]
        a0, b0, c0 = row[0:1], row[1:2], row[2:3]
        a1, b1, c1 = row[3:4], row[4:5], row[5:6]
        if d == 0:
            g, h = a0, c0
            p, q = a1, c1
        else:
            denom = 1.0 - b0 * q_prev
            g = (a0 + b0 * p_prev) / denom
            h = c0 / denom
            p = a1 + b1 * p_prev + b1 * q_prev * g
            q = c1 + b1 * q_prev * h
        gains.append((g, h, p, q))
        p_prev, q_prev = p, q
    later = jnp.zeros_like(gains[0][0])
    for d in range(count - 1, -1, -1):
        g, h, _, _ = gains[d]
        first = g + h * later
        if d > 0:
            _, _, p, q = gains[d - 1]
            before = p + q * first
        else:
            before = jnp.zeros_like(first)
        out_ref[d, 0:1, :] = before
        out_ref[d, 1:2, :] = later
        later = first


def reduced_solve(coef):
    count, _, m = coef.shape
    return pl.pallas_call(
        reduced_kernel, out_shape=jax.ShapeDtypeStruct((count, 2, m), coef.dtype)
    )(coef)


def solve_along_0(f, k, r, axis):
    count = lax.axis_size(axis)
    n, rows, lanes = f.shape
    a, b, c = local_solve(f, k, r)
    lines = rows * lanes
    m = lines // count
    coef = jnp.stack([a[0], b[0], c[0], a[n - 1], b[n - 1], c[n - 1]]).reshape(6, count, m)
    coef = jnp.transpose(coef, (1, 0, 2))
    gathered = lax.all_to_all(coef, axis, 0, 0, tiled=True)
    ends = reduced_solve(gathered)
    ends = lax.all_to_all(ends, axis, 0, 0, tiled=True)
    ends = jnp.transpose(ends, (1, 0, 2)).reshape(2, rows, lanes)
    return a + b * ends[0][None] + c * ends[1][None]


def per_device(source, coupling_x, coupling_y, reaction):
    halfway = solve_along_0(source, coupling_x, reaction, "gx")
    turned = solve_along_0(
        jnp.swapaxes(halfway, 0, 1),
        jnp.swapaxes(coupling_y, 0, 1),
        jnp.swapaxes(reaction, 0, 1),
        "gy",
    )
    return jnp.swapaxes(turned, 0, 1)


def solution(mesh):
    placed = (P("gx", "gy", None), P("gx", "gy", None), P("gx", "gy", None), P("gx", "gy", None))
    return jax.shard_map(
        per_device, mesh=mesh, in_specs=placed, out_specs=P("gx", "gy", None), check_vma=False
    )
```

time: 1010 us -> 136 us (0.13)
  blocking collectives: 877 us -> 79.8 us
  other arithmetic: 63.5 us -> 3.01 us
  local copies, waits for them, and re-layouts: 52.7 us -> 13.8 us
  waiting for transfers between devices: 0 us -> 25.7 us
    all_gather x22 -> x0, blocking collectives: 877 us -> none  [entering_2(): everything = jax.tree.map(lambda part: lax.all_gather(part, axis), x)]
    all_to_all x0 -> x3, blocking collectives: none -> 79.8 us  [the longest x2 69 us: solve_along_0(): gathered = lax.all_to_all(coef, axis, 0, 0, tiled=True)]
    select_n x240 -> x0, other arithmetic: 54.2 us -> none  [turn(): return jax.tree.map(lambda a, b: jnp.where(reached, a, b), new, before)]
    pad x110 -> x0, local copies, waits for them, and re-layouts: 42.1 us -> none  [the longest x90 40.2 us: solve_lines(): lax.associative_scan(lambda earlier, later: compose(later, earlier), cell...]
    all_to_all x0 -> x1, waiting for transfers between devices: none -> 25.7 us  [solve_along_0(): ends = lax.all_to_all(ends, axis, 0, 0, tiled=True)]
  transfers between devices with their start and end apart: 0 -> 1, of which waited for: 0 -> 1; matrix products, arithmetic and copies ran while one was open for 0% -> 1% of each run, Pallas kernels for 0% -> 0%
where the time goes in v1:
time: 136 us; the launch traced here: 135 us
  blocking collectives  79.8 us (59%)
  waiting for transfers between devices  25.7 us (19%)
  local copies, waits for them, and re-layouts  13.8 us (10%)
  Pallas kernels  8 us (6%)
  starting transfers between devices  4.7 us (3%)
  other arithmetic  3.01 us (2%)
    all_to_all x2, blocking collectives, solve_along_0(): gathered = lax.all_to_all(coef, axis, 0, 0, tiled=True)  69 us
    all_to_all x1, waiting for transfers between devices, solve_along_0(): ends = lax.all_to_all(ends, axis, 0, 0, tiled=True)  25.7 us
    all_to_all x1, blocking collectives, solve_along_0(): ends = lax.all_to_all(ends, axis, 0, 0, tiled=True)  10.8 us
    unnamed x32, local copies, waits for them, and re-layouts  9.62 us
    all_to_all x1, starting transfers between devices, solve_along_0(): ends = lax.all_to_all(ends, axis, 0, 0, tiled=True)  4.7 us
    pallas_call x2, Pallas kernels, reduced_solve(): pl.pallas_call(reduced_kernel, out_shape=jax.ShapeDtypeStruct((count, 2,...  4.59 us
    pallas_call x2, Pallas kernels, local_solve(): pl.pallas_call(local_kernel, out_shape=(shape, shape, shape))(f, k, r)  3.4 us
  transfers between devices with their start and end apart: 1, of which 1 were waited for; matrix products, arithmetic and copies ran while one was open for 1% of the time, Pallas kernels for 0%

profile of v1, /device:TPU:2, one launch (start us, length us, event | category | flops | bytes accessed | tf_op | source)
XLA Modules:
  0.0 135.0 jit_solution(9026715973404759102)
XLA Ops:
  0.0 1.7 %shard_map.46 = (f32[8,16,128]{2,1,0:T(8,128)}, f32[8,16,128]{2,1,0:T(8,128)}, f32[8,16,128]{2,1,0:T(8,128)}) custom-call(f32[8,16,128]{2,1,0:T(8,128)} %f_ref.1, f32[8,16,128]{2,1,0:T(8,128)} %k_ref.1, f32[8,16,128]{2,1,0:T(8,128)} %r_ref.1), custom_call_target="tpu_custom_call" | custom-call | tf_op jit(solution)/shard_map/pallas_call | solution.py:37
  1.7 0.7 constant_dynamic-update-slice_fusion.5
  2.4 0.7 constant_dynamic-update-slice_fusion.4
  3.1 0.7 constant_dynamic-update-slice_fusion.3
  3.8 0.7 constant_dynamic-update-slice_fusion.2
  4.5 0.0 copy-done.2
  4.5 0.7 constant_dynamic-update-slice_fusion
  5.2 0.1 reshape.16
  5.3 0.1 copy.34
  5.4 0.2 reshape.40
  5.6 55.5 %all_to_all.20 = f32[64,1,192]{2,1,0:T(1,128)S(1)} all-to-all(f32[64,1,192]{2,1,0:T(1,128)S(1)} %reshape.40), channel_id=1, replica_groups=mesh['gx'=64,'gy'=16] {'gx'}, dimensions={0} | all-to-all | bytes 98304 | tf_op jit(solution)/shard_map/all_to_all | solution.py:89
  61.1 0.6 broadcast.12
  61.7 0.8 reduce.16
  62.5 0.8 reshape.41.coef_ref
  63.3 2.8 %shard_map.47 = f32[64,2,32]{2,1,0:T(2,128)} custom-call(f32[64,6,32]{2,1,0:T(8,128)} %reshape.41.coef_ref), custom_call_target="tpu_custom_call" | custom-call | tf_op jit(solution)/shard_map/pallas_call | solution.py:76
  66.2 4.7 %all-to-all-start.1 = ((f32[64,2,32]{2,1,0:T(2,128)}), f32[64,2,32]{2,1,0:T(2,128)S(1)}, u32[]{:S(2)}, u32[]{:S(2)}) async-start(f32[64,2,32]{2,1,0:T(2,128)} %shard_map.47), calls=%async_computation.1 | async-start | bytes 131072 | tf_op jit(solution)/shard_map/all_to_all | solution.py:91
  70.9 0.0 copy-done
  70.9 0.0 copy-done.7
  70.9 0.7 copy_bitcast_fusion.2
  71.6 25.7 %all-to-all-done.1 = f32[64,2,32]{2,1,0:T(2,128)S(1)} async-done(((f32[64,2,32]{2,1,0:T(2,128)}), f32[64,2,32]{2,1,0:T(2,128)S(1)}, u32[]{:S(2)}, u32[]{:S(2)}) %all-to-all-start.1) | async-done | bytes 16416 | tf_op jit(solution)/shard_map/all_to_all | solution.py:91
  97.3 0.2 slice_reduce_fusion.1
  97.4 0.0 copy-start.1
  97.5 0.1 mul.40
  97.5 0.1 mul.43
  97.6 0.5 copy-done.3
  98.1 0.2 copy-done.1
  98.3 0.7 fusion.1.f_ref
  99.0 1.8 %shard_map.48 = (f32[16,8,128]{2,1,0:T(8,128)}, f32[16,8,128]{2,1,0:T(8,128)}, f32[16,8,128]{2,1,0:T(8,128)}) custom-call(f32[16,8,128]{2,1,0:T(8,128)} %fusion.1.f_ref, f32[16,8,128]{2,1,0:T(8,128)} %get-tuple-element.22.k_ref, f32[16,8,128]{2,1,0:T(8,128)} %get-tuple-element.21.r_ref), custom_call_target="tpu_custom_call" | custom-call | tf_op jit(solution)/shard_map/pallas_call | solution.py:37
  100.7 0.7 constant_dynamic-update-slice_fusion.11
  101.4 0.7 constant_dynamic-update-slice_fusion.10
  102.1 0.7 constant_dynamic-update-slice_fusion.9
  102.8 0.7 constant_dynamic-update-slice_fusion.8
  103.5 0.7 constant_dynamic-update-slice_fusion.7
  104.1 0.7 constant_dynamic-update-slice_fusion.6
  104.8 0.1 reshape.17
  104.9 0.1 reshape.42
  105.0 13.5 %all_to_all.21 = f32[16,1,384]{2,1,0:T(1,128)S(1)} all-to-all(f32[16,1,384]{2,1,0:T(1,128)S(1)} %reshape.42), channel_id=1, replica_groups=mesh['gx'=64,'gy'=16] {'gy'}, dimensions={0} | all-to-all | bytes 49152 | tf_op jit(solution)/shard_map/all_to_all | solution.py:89
  118.5 0.7 reduce.17
  119.3 0.7 reshape.43.coef_ref
  120.0 1.8 %shard_map.49 = f32[16,2,64]{2,1,0:T(2,128)} custom-call(f32[16,6,64]{2,1,0:T(8,128)} %reshape.43.coef_ref), custom_call_target="tpu_custom_call" | custom-call | tf_op jit(solution)/shard_map/pallas_call | solution.py:76
  121.8 0.8 reshape.44
  122.6 10.8 %all_to_all.22 = f32[16,1,128]{2,1,0:T(1,128)S(1)} all-to-all(f32[16,1,128]{2,1,0:T(1,128)S(1)} %reshape.44), channel_id=1, replica_groups=mesh['gx'=64,'gy'=16] {'gy'}, dimensions={0} | all-to-all | bytes 16384 | tf_op jit(solution)/shard_map/all_to_all | solution.py:91
  133.4 0.7 reduce.18
  134.1 0.1 reshape.45
  134.2 0.1 mul.46
  134.3 0.1 mul.49
  134.4 0.0 copy-done.4
  134.4 0.6 copy.18
  (13 shorter events, 0.1 us)
Async XLA Ops:
  1.7 2.8 %copy-start.2 = (f32[8,16,128]{2,1,0:T(8,128)S(1)}, f32[8,16,128]{2,1,0:T(8,128)}, u32[]{:S(2)}) copy-start(f32[8,16,128]{2,1,0:T(8,128)} %get-tuple-element.12) | copy-start | bytes 196612
  66.2 4.7 %copy-start = (f32[8,16,128]{2,1,0:T(8,128)S(1)}, f32[8,16,128]{2,1,0:T(8,128)}, u32[]{:S(2)}) copy-start(f32[8,16,128]{2,1,0:T(8,128)} %r_ref.1) | copy-start | bytes 196612
  66.2 4.7 %copy-start.7 = (f32[8,16,128]{2,1,0:T(8,128)S(1)}, f32[8,16,128]{2,1,0:T(8,128)}, u32[]{:S(2)}) copy-start(f32[8,16,128]{2,1,0:T(8,128)} %param.6) | copy-start | bytes 196612
  66.2 31.1 %all-to-all-start.1 = ((f32[64,2,32]{2,1,0:T(2,128)}), f32[64,2,32]{2,1,0:T(2,128)S(1)}, u32[]{:S(2)}, u32[]{:S(2)}) async-start(f32[64,2,32]{2,1,0:T(2,128)} %shard_map.47), calls=%async_computation.1 | async-start | bytes 131072 | tf_op jit(solution)/shard_map/all_to_all | solution.py:91
  97.3 0.8 copy-start.3
  97.4 0.8 copy-start.1
  120.0 14.4 %copy-start.6 = (f32[16,8,128]{2,1,0:T(8,128)S(1)}, f32[16,8,128]{2,1,0:T(8,128)}, u32[]{:S(2)}) copy-start(f32[16,8,128]{2,1,0:T(8,128)} %get-tuple-element.16) | copy-start | bytes 196612
  121.8 12.6 %copy-start.5 = (f32[16,8,128]{2,1,0:T(8,128)S(1)}, f32[16,8,128]{2,1,0:T(8,128)}, u32[]{:S(2)}) copy-start(f32[16,8,128]{2,1,0:T(8,128)} %get-tuple-element.15) | copy-start | bytes 196612
  122.6 11.8 %copy-start.4 = (f32[16,8,128]{2,1,0:T(8,128)S(1)}, f32[16,8,128]{2,1,0:T(8,128)}, u32[]{:S(2)}) copy-start(f32[16,8,128]{2,1,0:T(8,128)} %get-tuple-element.14) | copy-start | bytes 196612

commit v2 on v1

v2 whole, which is shorter than its diff:
```python
from functools import partial

import jax
import jax.numpy as jnp
from jax import lax
from jax.experimental import pallas as pl
from jax.sharding import PartitionSpec as P


def local_kernel(f_ref, k_ref, r_ref, a_ref, b_ref, c_ref, e_ref):
    n = f_ref.shape[0]
    zero = jnp.zeros(f_ref.shape[1:], f_ref.dtype)
    ratio, shifted, shifted_b = zero, zero, zero
    for i in range(n):
        link = k_ref[i]
        denom = r_ref[i] + 2.0 * link + link * ratio
        ratio = -link / denom
        shifted = (f_ref[i] + link * shifted) / denom
        shifted_b = (link if i == 0 else link * shifted_b) / denom
        a_ref[i] = shifted
        b_ref[i] = shifted_b
        c_ref[i] = ratio
    later_a = a_ref[n - 1]
    later_b = b_ref[n - 1]
    later_c = k_ref[n - 1] / denom
    c_ref[n - 1] = later_c
    for i in range(n - 2, -1, -1):
        ratio = c_ref[i]
        later_a = a_ref[i] - ratio * later_a
        later_b = b_ref[i] - ratio * later_b
        later_c = -ratio * later_c
        a_ref[i] = later_a
        b_ref[i] = later_b
        c_ref[i] = later_c
    for j, (ref, at) in enumerate(((a_ref, 0), (b_ref, 0), (c_ref, 0), (a_ref, n - 1), (b_ref, n - 1), (c_ref, n - 1))):
        e_ref[j] = ref[at]


def local_solve(f, k, r):
    shape = jax.ShapeDtypeStruct(f.shape, f.dtype)
    ends = jax.ShapeDtypeStruct((6,) + f.shape[1:], f.dtype)
    return pl.pallas_call(local_kernel, out_shape=(shape, shape, shape, ends))(f, k, r)


def compose(earlier, later):
    xa0, xb0, xc0, xa1, xb1, xc1 = earlier
    ya0, yb0, yc0, ya1, yb1, yc1 = later
    denom = 1.0 - xc1 * yb0
    join_a = (xa1 + xc1 * ya0) / denom
    join_b = xb1 / denom
    join_c = xc1 * yc0 / denom
    next_a = ya0 + yb0 * join_a
    next_b = yb0 * join_b
    next_c = yc0 + yb0 * join_c
    return (
        xa0 + xc0 * next_a,
        xb0 + xc0 * next_b,
        xc0 * next_c,
        ya1 + yb1 * join_a,
        yb1 * join_b,
        yc1 + yb1 * join_c,
    )


def round_kernel(final, left_ref, right_ref, ip_ref, ep_ref, is_ref, es_ref, *rest):
    rows = lambda ref: tuple(ref[i] for i in range(6))
    from_left, from_right = rows(left_ref), rows(right_ref)
    incl_pre = compose(from_left, rows(ip_ref))
    excl_pre = compose(from_left, rows(ep_ref))
    incl_suf = compose(rows(is_ref), from_right)
    excl_suf = compose(rows(es_ref), from_right)
    if not final:
        for out_ref, value in zip(rest, (incl_pre, excl_pre, incl_suf, excl_suf)):
            for i in range(6):
                out_ref[i] = value[i]
        return
    a_ref, b_ref, c_ref, out_ref = rest
    q = excl_pre[5]
    before = (excl_pre[3] + q * incl_suf[0]) / (1.0 - q * incl_suf[1])
    v = excl_suf[1]
    after = (excl_suf[0] + v * incl_pre[3]) / (1.0 - v * incl_pre[5])
    for i in range(a_ref.shape[0]):
        out_ref[i] = a_ref[i] + b_ref[i] * before + c_ref[i] * after


def solve_along_0(f, k, r, axis):
    count = lax.axis_size(axis)
    a, b, c, block = local_solve(f, k, r)
    if count == 1:
        return a
    identity = jnp.zeros_like(block).at[2].set(1.0).at[4].set(1.0)
    incl_pre, excl_pre, incl_suf, excl_suf = block, identity, block, identity
    state = jax.ShapeDtypeStruct(block.shape, block.dtype)
    shift = 1
    while shift < count:
        rightward = [(i, i + shift) for i in range(count - shift)]
        leftward = [(i + shift, i) for i in range(count - shift)]
        from_left = lax.ppermute(incl_pre, axis, rightward)
        from_right = lax.ppermute(incl_suf, axis, leftward)
        final = shift * 2 >= count
        operands = (from_left, from_right, incl_pre, excl_pre, incl_suf, excl_suf)
        if final:
            return pl.pallas_call(
                partial(round_kernel, True), out_shape=jax.ShapeDtypeStruct(a.shape, a.dtype)
            )(*operands, a, b, c)
        incl_pre, excl_pre, incl_suf, excl_suf = pl.pallas_call(
            partial(round_kernel, False), out_shape=(state, state, state, state)
        )(*operands)
        shift *= 2


def per_device(source, coupling_x, coupling_y, reaction):
    halfway = solve_along_0(source, coupling_x, reaction, "gx")
    turned = solve_along_0(
        jnp.swapaxes(halfway, 0, 1),
        jnp.swapaxes(coupling_y, 0, 1),
        jnp.swapaxes(reaction, 0, 1),
        "gy",
    )
    return jnp.swapaxes(turned, 0, 1)


def solution(mesh):
    placed = (P("gx", "gy", None), P("gx", "gy", None), P("gx", "gy", None), P("gx", "gy", None))
    return jax.shard_map(
        per_device, mesh=mesh, in_specs=placed, out_specs=P("gx", "gy", None), check_vma=False
    )
```

time: 136 us -> 194 us (1.43)
  blocking collectives: 79.8 us -> 0 us
  starting transfers between devices: 4.7 us -> 81.6 us
  waiting for transfers between devices: 25.7 us -> 80.9 us
  Pallas kernels: 8 us -> 19.4 us
  local copies, waits for them, and re-layouts: 13.8 us -> 10.3 us
  other arithmetic: 3.01 us -> 0 us
    ppermute x0 -> x20, starting transfers between devices: none -> 81.6 us  [the longest x10 67.4 us: solve_along_0(): from_left = lax.ppermute(incl_pre, axis, rightward)]
    ppermute x0 -> x20, waiting for transfers between devices: none -> 80.9 us  [the longest x10 76.5 us: solve_along_0(): from_right = lax.ppermute(incl_suf, axis, leftward)]
    all_to_all x3 -> x0, blocking collectives: 79.8 us -> none  [the longest x2 69 us: solve_along_0(): gathered = lax.all_to_all(coef, axis, 0, 0, tiled=True)]
    all_to_all x1 -> x0, waiting for transfers between devices: 25.7 us -> none  [solve_along_0(): ends = lax.all_to_all(ends, axis, 0, 0, tiled=True)]
    pallas_call x4 -> x12, Pallas kernels: 8 us -> 19.4 us  [the longest x8 12.5 us: solve_along_0(): pl.pallas_call(partial(round_kernel, False), out_shape=(state, state, sta...]
    all_to_all x1 -> x0, starting transfers between devices: 4.7 us -> none  [solve_along_0(): ends = lax.all_to_all(ends, axis, 0, 0, tiled=True)]
    all_to_all x3 -> x0, other arithmetic: 2.3 us -> none  [the longest x2 1.59 us: solve_along_0(): gathered = lax.all_to_all(coef, axis, 0, 0, tiled=True)]
    unnamed x32 -> x46, local copies, waits for them, and re-layouts: 9.62 us -> 7.37 us
  transfers between devices with their start and end apart: 1 -> 20, of which waited for: 1 -> 18; matrix products, arithmetic and copies ran while one was open for 1% -> 1% of each run, Pallas kernels for 0% -> 0%
where the time goes in v2:
time: 194 us; the launch traced here: 192 us
  starting transfers between devices  81.6 us (42%)
  waiting for transfers between devices  80.9 us (42%)
  Pallas kernels  19.4 us (10%)
  local copies, waits for them, and re-layouts  10.3 us (5%)
    ppermute x10, waiting for transfers between devices, solve_along_0(): from_right = lax.ppermute(incl_suf, axis, leftward)  76.5 us
    ppermute x10, starting transfers between devices, solve_along_0(): from_left = lax.ppermute(incl_pre, axis, rightward)  67.4 us
    ppermute x10, starting transfers between devices, solve_along_0(): from_right = lax.ppermute(incl_suf, axis, leftward)  14.2 us
    pallas_call x8, Pallas kernels, solve_along_0(): pl.pallas_call(partial(round_kernel, False), out_shape=(state, state, sta...  12.5 us
    unnamed x46, local copies, waits for them, and re-layouts  7.37 us
    ppermute x10, waiting for transfers between devices, solve_along_0(): from_left = lax.ppermute(incl_pre, axis, rightward)  4.33 us
  transfers between devices with their start and end apart: 20, of which 18 were waited for; matrix products, arithmetic and copies ran while one was open for 1% of the time, Pallas kernels for 0%

profile of v2, /device:TPU:2, one launch (start us, length us, event | category | flops | bytes accessed | tf_op | source)
XLA Modules:
  0.0 192.5 jit_solution(15067445948808607644)
XLA Ops:
  0.0 1.7 shard_map.46
  1.7 1.7 collective-permute-start
  3.4 1.3 collective-permute-start.1
  4.7 3.7 %collective-permute-done.1.right_ref = f32[6,16,128]{2,1,0:T(8,128)S(1)} collective-permute-done((f32[6,16,128]{2,1,0:T(8,128)}, f32[6,16,128]{2,1,0:T(8,128)S(1)}, u32[]{:S(2)}, u32[]{:S(2)}) %collective-permute-start.1) | collective-permute-done | bytes 49184 | tf_op jit(solution)/shard_map/ppermute | solution.py:99
  9.1 1.6 shard_map.47
  10.7 4.6 %collective-permute-start.2 = (f32[6,16,128]{2,1,0:T(8,128)}, f32[6,16,128]{2,1,0:T(8,128)S(1)}, u32[]{:S(2)}, u32[]{:S(2)}) collective-permute-start(f32[6,16,128]{2,1,0:T(8,128)} %get-tuple-element.94.ip_ref), channel_id=1, source_target_pairs={{0,32},{16,48},{32,64},{48,80},{64,96},{80,112},{96,128},{112,144}... | collective-permute-start | bytes 147464 | tf_op jit(solution)/shard_map/ppermute | solution.py:98
  15.3 1.3 collective-permute-start.3
  16.6 0.7 collective-permute-done.2.left_ref
  17.4 4.1 %collective-permute-done.3.right_ref = f32[6,16,128]{2,1,0:T(8,128)S(1)} collective-permute-done((f32[6,16,128]{2,1,0:T(8,128)}, f32[6,16,128]{2,1,0:T(8,128)S(1)}, u32[]{:S(2)}, u32[]{:S(2)}) %collective-permute-start.3) | collective-permute-done | bytes 49184 | tf_op jit(solution)/shard_map/ppermute | solution.py:99
  22.1 1.6 shard_map.48
  23.8 7.5 %collective-permute-start.4 = (f32[6,16,128]{2,1,0:T(8,128)}, f32[6,16,128]{2,1,0:T(8,128)S(1)}, u32[]{:S(2)}, u32[]{:S(2)}) collective-permute-start(f32[6,16,128]{2,1,0:T(8,128)} %get-tuple-element.98.ip_ref), channel_id=1, source_target_pairs={{0,64},{16,80},{32,96},{48,112},{64,128},{80,144},{96,160},{112,17... | collective-permute-start | bytes 147464 | tf_op jit(solution)/shard_map/ppermute | solution.py:98
  31.3 1.3 collective-permute-start.5
  32.6 0.8 collective-permute-done.4.left_ref
  33.3 5.0 %collective-permute-done.5.right_ref = f32[6,16,128]{2,1,0:T(8,128)S(1)} collective-permute-done((f32[6,16,128]{2,1,0:T(8,128)}, f32[6,16,128]{2,1,0:T(8,128)S(1)}, u32[]{:S(2)}, u32[]{:S(2)}) %collective-permute-start.5) | collective-permute-done | bytes 49184 | tf_op jit(solution)/shard_map/ppermute | solution.py:99
  39.0 1.6 shard_map.49
  40.6 9.1 %collective-permute-start.6 = (f32[6,16,128]{2,1,0:T(8,128)}, f32[6,16,128]{2,1,0:T(8,128)S(1)}, u32[]{:S(2)}, u32[]{:S(2)}) collective-permute-start(f32[6,16,128]{2,1,0:T(8,128)} %get-tuple-element.102.ip_ref), channel_id=1, source_target_pairs={{0,128},{16,144},{32,160},{48,176},{64,192},{80,208},{96,224},{112... | collective-permute-start | bytes 147464 | tf_op jit(solution)/shard_map/ppermute | solution.py:98
  49.7 1.3 collective-permute-start.7
  51.0 0.7 collective-permute-done.6.left_ref
  51.7 9.3 %collective-permute-done.7.right_ref = f32[6,16,128]{2,1,0:T(8,128)S(1)} collective-permute-done((f32[6,16,128]{2,1,0:T(8,128)}, f32[6,16,128]{2,1,0:T(8,128)S(1)}, u32[]{:S(2)}, u32[]{:S(2)}) %collective-permute-start.7) | collective-permute-done | bytes 49184 | tf_op jit(solution)/shard_map/ppermute | solution.py:99
  61.6 1.6 shard_map.50
  63.3 15.4 %collective-permute-start.8 = (f32[6,16,128]{2,1,0:T(8,128)}, f32[6,16,128]{2,1,0:T(8,128)S(1)}, u32[]{:S(2)}, u32[]{:S(2)}) collective-permute-start(f32[6,16,128]{2,1,0:T(8,128)} %get-tuple-element.106.ip_ref), channel_id=1, source_target_pairs={{0,256},{16,272},{32,288},{48,304},{64,320},{80,336},{96,352},{112... | collective-permute-start | bytes 147464 | tf_op jit(solution)/shard_map/ppermute | solution.py:98
  78.6 1.3 collective-permute-start.9
  79.9 0.7 collective-permute-done.8.left_ref
  80.7 13.3 %collective-permute-done.9.right_ref = f32[6,16,128]{2,1,0:T(8,128)S(1)} collective-permute-done((f32[6,16,128]{2,1,0:T(8,128)}, f32[6,16,128]{2,1,0:T(8,128)S(1)}, u32[]{:S(2)}, u32[]{:S(2)}) %collective-permute-start.9) | collective-permute-done | bytes 49184 | tf_op jit(solution)/shard_map/ppermute | solution.py:99
  94.6 1.6 shard_map.51
  96.3 12.9 %collective-permute-start.10 = (f32[6,16,128]{2,1,0:T(8,128)}, f32[6,16,128]{2,1,0:T(8,128)S(1)}, u32[]{:S(2)}, u32[]{:S(2)}) collective-permute-start(f32[6,16,128]{2,1,0:T(8,128)} %get-tuple-element.110.ip_ref), channel_id=1, source_target_pairs={{0,512},{16,528},{32,544},{48,560},{64,576},{80,592},{96,608},{112... | collective-permute-start | bytes 147464 | tf_op jit(solution)/shard_map/ppermute | solution.py:98
  109.2 1.4 collective-permute-start.11
  111.9 21.9 %collective-permute-done.11.right_ref = f32[6,16,128]{2,1,0:T(8,128)S(1)} collective-permute-done((f32[6,16,128]{2,1,0:T(8,128)}, f32[6,16,128]{2,1,0:T(8,128)S(1)}, u32[]{:S(2)}, u32[]{:S(2)}) %collective-permute-start.11) | collective-permute-done | bytes 49184 | tf_op jit(solution)/shard_map/ppermute | solution.py:99
  134.5 1.7 shard_map.52
  136.2 1.5 copy.14
  137.7 1.8 shard_map.53
  139.4 3.4 %collective-permute-start.12 = (f32[6,8,128]{2,1,0:T(8,128)}, f32[6,8,128]{2,1,0:T(8,128)S(1)}, u32[]{:S(2)}, u32[]{:S(2)}) collective-permute-start(f32[6,8,128]{2,1,0:T(8,128)} %get-tuple-element.117.ip_ref.is_ref), channel_id=1, source_target_pairs={{0,1},{1,2},{2,3},{3,4},{4,5},{5,6},{6,7},{7,8},{8,9},{9,10},{10,1... | collective-permute-start | bytes 73736 | tf_op jit(solution)/shard_map/ppermute | solution.py:98
  142.8 2.4 %collective-permute-start.13 = (f32[6,8,128]{2,1,0:T(8,128)}, f32[6,8,128]{2,1,0:T(8,128)S(1)}, u32[]{:S(2)}, u32[]{:S(2)}) collective-permute-start(f32[6,8,128]{2,1,0:T(8,128)} %get-tuple-element.117.ip_ref.is_ref), channel_id=1, source_target_pairs={{1,0},{2,1},{3,2},{4,3},{5,4},{6,5},{7,6},{8,7},{9,8},{10,9},{11,1... | collective-permute-start | bytes 73736 | tf_op jit(solution)/shard_map/ppermute | solution.py:99
  145.4 3.4 %collective-permute-done.13.right_ref = f32[6,8,128]{2,1,0:T(8,128)S(1)} collective-permute-done((f32[6,8,128]{2,1,0:T(8,128)}, f32[6,8,128]{2,1,0:T(8,128)S(1)}, u32[]{:S(2)}, u32[]{:S(2)}) %collective-permute-start.13) | collective-permute-done | bytes 24608 | tf_op jit(solution)/shard_map/ppermute | solution.py:99
  149.4 1.5 shard_map.54
  150.9 6.1 %collective-permute-start.14 = (f32[6,8,128]{2,1,0:T(8,128)}, f32[6,8,128]{2,1,0:T(8,128)S(1)}, u32[]{:S(2)}, u32[]{:S(2)}) collective-permute-start(f32[6,8,128]{2,1,0:T(8,128)} %get-tuple-element.118.ip_ref), channel_id=1, source_target_pairs={{0,2},{1,3},{2,4},{3,5},{4,6},{5,7},{6,8},{7,9},{8,10},{9,11},{10,... | collective-permute-start | bytes 73736 | tf_op jit(solution)/shard_map/ppermute | solution.py:98
  157.0 1.3 collective-permute-start.15
  158.7 5.7 %collective-permute-done.15.right_ref = f32[6,8,128]{2,1,0:T(8,128)S(1)} collective-permute-done((f32[6,8,128]{2,1,0:T(8,128)}, f32[6,8,128]{2,1,0:T(8,128)S(1)}, u32[]{:S(2)}, u32[]{:S(2)}) %collective-permute-start.15) | collective-permute-done | bytes 24608 | tf_op jit(solution)/shard_map/ppermute | solution.py:99
  165.0 1.5 shard_map.55
  166.5 3.5 %collective-permute-start.16 = (f32[6,8,128]{2,1,0:T(8,128)}, f32[6,8,128]{2,1,0:T(8,128)S(1)}, u32[]{:S(2)}, u32[]{:S(2)}) collective-permute-start(f32[6,8,128]{2,1,0:T(8,128)} %get-tuple-element.122.ip_ref), channel_id=1, source_target_pairs={{0,4},{1,5},{2,6},{3,7},{4,8},{5,9},{6,10},{7,11},{8,12},{9,13},{1... | collective-permute-start | bytes 73736 | tf_op jit(solution)/shard_map/ppermute | solution.py:98
  170.0 1.3 collective-permute-start.17
  171.7 4.2 %collective-permute-done.17.right_ref = f32[6,8,128]{2,1,0:T(8,128)S(1)} collective-permute-done((f32[6,8,128]{2,1,0:T(8,128)}, f32[6,8,128]{2,1,0:T(8,128)S(1)}, u32[]{:S(2)}, u32[]{:S(2)}) %collective-permute-start.17) | collective-permute-done | bytes 24608 | tf_op jit(solution)/shard_map/ppermute | solution.py:99
  176.5 1.5 shard_map.56
  178.0 3.2 %collective-permute-start.18 = (f32[6,8,128]{2,1,0:T(8,128)}, f32[6,8,128]{2,1,0:T(8,128)S(1)}, u32[]{:S(2)}, u32[]{:S(2)}) collective-permute-start(f32[6,8,128]{2,1,0:T(8,128)} %get-tuple-element.126.ip_ref), channel_id=1, source_target_pairs={{0,8},{1,9},{2,10},{3,11},{4,12},{5,13},{6,14},{7,15},{16,24},{17,... | collective-permute-start | bytes 73736 | tf_op jit(solution)/shard_map/ppermute | solution.py:98
  181.3 1.3 collective-permute-start.19
  183.0 5.7 %collective-permute-done.19.right_ref = f32[6,8,128]{2,1,0:T(8,128)S(1)} collective-permute-done((f32[6,8,128]{2,1,0:T(8,128)}, f32[6,8,128]{2,1,0:T(8,128)S(1)}, u32[]{:S(2)}, u32[]{:S(2)}) %collective-permute-start.19) | collective-permute-done | bytes 24608 | tf_op jit(solution)/shard_map/ppermute | solution.py:99
  189.3 1.7 shard_map.57
  191.0 1.5 copy.8
  (52 shorter events, 8.7 us)
Async XLA Ops:
  1.7 3.0 %collective-permute-start = (f32[6,16,128]{2,1,0:T(8,128)}, f32[6,16,128]{2,1,0:T(8,128)S(1)}, u32[]{:S(2)}, u32[]{:S(2)}) collective-permute-start(f32[6,16,128]{2,1,0:T(8,128)} %get-tuple-element.93.ip_ref.is_ref), channel_id=1, source_target_pairs={{0,16},{16,32},{32,48},{48,64},{64,80},{80,96},{96,112},{112,128},... | collective-permute-start | bytes 147464 | tf_op jit(solution)/shard_map/ppermute | solution.py:98
  3.4 5.0 %collective-permute-start.1 = (f32[6,16,128]{2,1,0:T(8,128)}, f32[6,16,128]{2,1,0:T(8,128)S(1)}, u32[]{:S(2)}, u32[]{:S(2)}) collective-permute-start(f32[6,16,128]{2,1,0:T(8,128)} %get-tuple-element.93.ip_ref.is_ref), channel_id=1, source_target_pairs={{16,0},{32,16},{48,32},{64,48},{80,64},{96,80},{112,96},{128,112},... | collective-permute-start | bytes 147464 | tf_op jit(solution)/shard_map/ppermute | solution.py:99
  4.7 3.7 %copy-start.8 = (f32[6,16,128]{2,1,0:T(8,128)}, f32[6,16,128]{2,1,0:T(8,128)S(1)}, u32[]{:S(2)}) copy-start(f32[6,16,128]{2,1,0:T(8,128)S(1)} %collective-permute-done.left_ref) | copy-start | bytes 147460
  8.5 0.6 copy-start.13
  10.7 6.7 %collective-permute-start.2 = (f32[6,16,128]{2,1,0:T(8,128)}, f32[6,16,128]{2,1,0:T(8,128)S(1)}, u32[]{:S(2)}, u32[]{:S(2)}) collective-permute-start(f32[6,16,128]{2,1,0:T(8,128)} %get-tuple-element.94.ip_ref), channel_id=1, source_target_pairs={{0,32},{16,48},{32,64},{48,80},{64,96},{80,112},{96,128},{112,144}... | collective-permute-start | bytes 147464 | tf_op jit(solution)/shard_map/ppermute | solution.py:98
  15.3 6.2 %collective-permute-start.3 = (f32[6,16,128]{2,1,0:T(8,128)}, f32[6,16,128]{2,1,0:T(8,128)S(1)}, u32[]{:S(2)}, u32[]{:S(2)}) collective-permute-start(f32[6,16,128]{2,1,0:T(8,128)} %get-tuple-element.95.is_ref), channel_id=1, source_target_pairs={{32,0},{48,16},{64,32},{80,48},{96,64},{112,80},{128,96},{144,112}... | collective-permute-start | bytes 147464 | tf_op jit(solution)/shard_map/ppermute | solution.py:99
  17.4 4.2 %copy-start.3 = (f32[6,16,128]{2,1,0:T(8,128)}, f32[6,16,128]{2,1,0:T(8,128)S(1)}, u32[]{:S(2)}) copy-start(f32[6,16,128]{2,1,0:T(8,128)S(1)} %collective-permute-done.2.left_ref) | copy-start | bytes 147460
  21.5 0.6 copy-start.9
  23.8 9.6 %collective-permute-start.4 = (f32[6,16,128]{2,1,0:T(8,128)}, f32[6,16,128]{2,1,0:T(8,128)S(1)}, u32[]{:S(2)}, u32[]{:S(2)}) collective-permute-start(f32[6,16,128]{2,1,0:T(8,128)} %get-tuple-element.98.ip_ref), channel_id=1, source_target_pairs={{0,64},{16,80},{32,96},{48,112},{64,128},{80,144},{96,160},{112,17... | collective-permute-start | bytes 147464 | tf_op jit(solution)/shard_map/ppermute | solution.py:98
  31.3 7.1 %collective-permute-start.5 = (f32[6,16,128]{2,1,0:T(8,128)}, f32[6,16,128]{2,1,0:T(8,128)S(1)}, u32[]{:S(2)}, u32[]{:S(2)}) collective-permute-start(f32[6,16,128]{2,1,0:T(8,128)} %get-tuple-element.99.is_ref), channel_id=1, source_target_pairs={{64,0},{80,16},{96,32},{112,48},{128,64},{144,80},{160,96},{176,11... | collective-permute-start | bytes 147464 | tf_op jit(solution)/shard_map/ppermute | solution.py:99
  33.3 5.0 %copy-start.4 = (f32[6,16,128]{2,1,0:T(8,128)}, f32[6,16,128]{2,1,0:T(8,128)S(1)}, u32[]{:S(2)}) copy-start(f32[6,16,128]{2,1,0:T(8,128)S(1)} %collective-permute-done.4.left_ref) | copy-start | bytes 147460
  38.4 0.6 copy-start.10
  40.6 11.1 %collective-permute-start.6 = (f32[6,16,128]{2,1,0:T(8,128)}, f32[6,16,128]{2,1,0:T(8,128)S(1)}, u32[]{:S(2)}, u32[]{:S(2)}) collective-permute-start(f32[6,16,128]{2,1,0:T(8,128)} %get-tuple-element.102.ip_ref), channel_id=1, source_target_pairs={{0,128},{16,144},{32,160},{48,176},{64,192},{80,208},{96,224},{112... | collective-permute-start | bytes 147464 | tf_op jit(solution)/shard_map/ppermute | solution.py:98
  49.7 11.4 %collective-permute-start.7 = (f32[6,16,128]{2,1,0:T(8,128)}, f32[6,16,128]{2,1,0:T(8,128)S(1)}, u32[]{:S(2)}, u32[]{:S(2)}) collective-permute-start(f32[6,16,128]{2,1,0:T(8,128)} %get-tuple-element.103.is_ref), channel_id=1, source_target_pairs={{128,0},{144,16},{160,32},{176,48},{192,64},{208,80},{224,96},{240... | collective-permute-start | bytes 147464 | tf_op jit(solution)/shard_map/ppermute | solution.py:99
  51.7 9.3 %copy-start.5 = (f32[6,16,128]{2,1,0:T(8,128)}, f32[6,16,128]{2,1,0:T(8,128)S(1)}, u32[]{:S(2)}) copy-start(f32[6,16,128]{2,1,0:T(8,128)S(1)} %collective-permute-done.6.left_ref) | copy-start | bytes 147460
  61.0 0.6 copy-start.11
  63.3 17.4 %collective-permute-start.8 = (f32[6,16,128]{2,1,0:T(8,128)}, f32[6,16,128]{2,1,0:T(8,128)S(1)}, u32[]{:S(2)}, u32[]{:S(2)}) collective-permute-start(f32[6,16,128]{2,1,0:T(8,128)} %get-tuple-element.106.ip_ref), channel_id=1, source_target_pairs={{0,256},{16,272},{32,288},{48,304},{64,320},{80,336},{96,352},{112... | collective-permute-start | bytes 147464 | tf_op jit(solution)/shard_map/ppermute | solution.py:98
  78.6 15.4 %collective-permute-start.9 = (f32[6,16,128]{2,1,0:T(8,128)}, f32[6,16,128]{2,1,0:T(8,128)S(1)}, u32[]{:S(2)}, u32[]{:S(2)}) collective-permute-start(f32[6,16,128]{2,1,0:T(8,128)} %get-tuple-element.107.is_ref), channel_id=1, source_target_pairs={{256,0},{272,16},{288,32},{304,48},{320,64},{336,80},{352,96},{368... | collective-permute-start | bytes 147464 | tf_op jit(solution)/shard_map/ppermute | solution.py:99
  80.7 13.4 %copy-start.6 = (f32[6,16,128]{2,1,0:T(8,128)}, f32[6,16,128]{2,1,0:T(8,128)S(1)}, u32[]{:S(2)}) copy-start(f32[6,16,128]{2,1,0:T(8,128)S(1)} %collective-permute-done.8.left_ref) | copy-start | bytes 147460
  94.0 0.6 copy-start.12
  94.6 16.0 %copy-start = (f32[8,16,128]{2,1,0:T(8,128)S(1)}, f32[8,16,128]{2,1,0:T(8,128)}, u32[]{:S(2)}) copy-start(f32[8,16,128]{2,1,0:T(8,128)} %r_ref.1) | copy-start | bytes 196612
  96.3 15.7 %collective-permute-start.10 = (f32[6,16,128]{2,1,0:T(8,128)}, f32[6,16,128]{2,1,0:T(8,128)S(1)}, u32[]{:S(2)}, u32[]{:S(2)}) collective-permute-start(f32[6,16,128]{2,1,0:T(8,128)} %get-tuple-element.110.ip_ref), channel_id=1, source_target_pairs={{0,512},{16,528},{32,544},{48,560},{64,576},{80,592},{96,608},{112... | collective-permute-start | bytes 147464 | tf_op jit(solution)/shard_map/ppermute | solution.py:98
  109.2 2.1 %copy-start.1 = (f32[8,16,128]{2,1,0:T(8,128)S(1)}, f32[8,16,128]{2,1,0:T(8,128)}, u32[]{:S(2)}) copy-start(f32[8,16,128]{2,1,0:T(8,128)} %param.14) | copy-start | bytes 196612
  109.2 24.7 %collective-permute-start.11 = (f32[6,16,128]{2,1,0:T(8,128)}, f32[6,16,128]{2,1,0:T(8,128)S(1)}, u32[]{:S(2)}, u32[]{:S(2)}) collective-permute-start(f32[6,16,128]{2,1,0:T(8,128)} %get-tuple-element.111.is_ref), channel_id=1, source_target_pairs={{512,0},{528,16},{544,32},{560,48},{576,64},{592,80},{608,96},{624... | collective-permute-start | bytes 147464 | tf_op jit(solution)/shard_map/ppermute | solution.py:99
  111.9 21.9 %copy-start.2 = (f32[6,16,128]{2,1,0:T(8,128)}, f32[6,16,128]{2,1,0:T(8,128)S(1)}, u32[]{:S(2)}) copy-start(f32[6,16,128]{2,1,0:T(8,128)S(1)} %collective-permute-done.10.left_ref) | copy-start | bytes 147460
  133.9 0.6 copy-start.7
  139.4 5.9 %collective-permute-start.12 = (f32[6,8,128]{2,1,0:T(8,128)}, f32[6,8,128]{2,1,0:T(8,128)S(1)}, u32[]{:S(2)}, u32[]{:S(2)}) collective-permute-start(f32[6,8,128]{2,1,0:T(8,128)} %get-tuple-element.117.ip_ref.is_ref), channel_id=1, source_target_pairs={{0,1},{1,2},{2,3},{3,4},{4,5},{5,6},{6,7},{7,8},{8,9},{9,10},{10,1... | collective-permute-start | bytes 73736 | tf_op jit(solution)/shard_map/ppermute | solution.py:98
  142.8 5.9 %collective-permute-start.13 = (f32[6,8,128]{2,1,0:T(8,128)}, f32[6,8,128]{2,1,0:T(8,128)S(1)}, u32[]{:S(2)}, u32[]{:S(2)}) collective-permute-start(f32[6,8,128]{2,1,0:T(8,128)} %get-tuple-element.117.ip_ref.is_ref), channel_id=1, source_target_pairs={{1,0},{2,1},{3,2},{4,3},{5,4},{6,5},{7,6},{8,7},{9,8},{10,9},{11,1... | collective-permute-start | bytes 73736 | tf_op jit(solution)/shard_map/ppermute | solution.py:99
  145.4 3.4 %copy-start.17 = (f32[6,8,128]{2,1,0:T(8,128)}, f32[6,8,128]{2,1,0:T(8,128)S(1)}, u32[]{:S(2)}) copy-start(f32[6,8,128]{2,1,0:T(8,128)S(1)} %collective-permute-done.12.left_ref) | copy-start | bytes 73732
  148.8 0.6 copy-start.21
  150.9 7.8 %collective-permute-start.14 = (f32[6,8,128]{2,1,0:T(8,128)}, f32[6,8,128]{2,1,0:T(8,128)S(1)}, u32[]{:S(2)}, u32[]{:S(2)}) collective-permute-start(f32[6,8,128]{2,1,0:T(8,128)} %get-tuple-element.118.ip_ref), channel_id=1, source_target_pairs={{0,2},{1,3},{2,4},{3,5},{4,6},{5,7},{6,8},{7,9},{8,10},{9,11},{10,... | collective-permute-start | bytes 73736 | tf_op jit(solution)/shard_map/ppermute | solution.py:98
  157.0 7.4 %collective-permute-start.15 = (f32[6,8,128]{2,1,0:T(8,128)}, f32[6,8,128]{2,1,0:T(8,128)S(1)}, u32[]{:S(2)}, u32[]{:S(2)}) collective-permute-start(f32[6,8,128]{2,1,0:T(8,128)} %get-tuple-element.119.is_ref), channel_id=1, source_target_pairs={{2,0},{3,1},{4,2},{5,3},{6,4},{7,5},{8,6},{9,7},{10,8},{11,9},{12,... | collective-permute-start | bytes 73736 | tf_op jit(solution)/shard_map/ppermute | solution.py:99
  158.7 5.7 %copy-start.14 = (f32[6,8,128]{2,1,0:T(8,128)}, f32[6,8,128]{2,1,0:T(8,128)S(1)}, u32[]{:S(2)}) copy-start(f32[6,8,128]{2,1,0:T(8,128)S(1)} %collective-permute-done.14.left_ref) | copy-start | bytes 73732
  164.4 0.6 copy-start.18
  166.5 5.2 %collective-permute-start.16 = (f32[6,8,128]{2,1,0:T(8,128)}, f32[6,8,128]{2,1,0:T(8,128)S(1)}, u32[]{:S(2)}, u32[]{:S(2)}) collective-permute-start(f32[6,8,128]{2,1,0:T(8,128)} %get-tuple-element.122.ip_ref), channel_id=1, source_target_pairs={{0,4},{1,5},{2,6},{3,7},{4,8},{5,9},{6,10},{7,11},{8,12},{9,13},{1... | collective-permute-start | bytes 73736 | tf_op jit(solution)/shard_map/ppermute | solution.py:98
  170.0 5.9 %collective-permute-start.17 = (f32[6,8,128]{2,1,0:T(8,128)}, f32[6,8,128]{2,1,0:T(8,128)S(1)}, u32[]{:S(2)}, u32[]{:S(2)}) collective-permute-start(f32[6,8,128]{2,1,0:T(8,128)} %get-tuple-element.123.is_ref), channel_id=1, source_target_pairs={{4,0},{5,1},{6,2},{7,3},{8,4},{9,5},{10,6},{11,7},{12,8},{13,9},{1... | collective-permute-start | bytes 73736 | tf_op jit(solution)/shard_map/ppermute | solution.py:99
  171.7 4.2 %copy-start.15 = (f32[6,8,128]{2,1,0:T(8,128)}, f32[6,8,128]{2,1,0:T(8,128)S(1)}, u32[]{:S(2)}) copy-start(f32[6,8,128]{2,1,0:T(8,128)S(1)} %collective-permute-done.16.left_ref) | copy-start | bytes 73732
  175.9 0.6 copy-start.19
  178.0 5.0 %collective-permute-start.18 = (f32[6,8,128]{2,1,0:T(8,128)}, f32[6,8,128]{2,1,0:T(8,128)S(1)}, u32[]{:S(2)}, u32[]{:S(2)}) collective-permute-start(f32[6,8,128]{2,1,0:T(8,128)} %get-tuple-element.126.ip_ref), channel_id=1, source_target_pairs={{0,8},{1,9},{2,10},{3,11},{4,12},{5,13},{6,14},{7,15},{16,24},{17,... | collective-permute-start | bytes 73736 | tf_op jit(solution)/shard_map/ppermute | solution.py:98
  181.3 7.4 %collective-permute-start.19 = (f32[6,8,128]{2,1,0:T(8,128)}, f32[6,8,128]{2,1,0:T(8,128)S(1)}, u32[]{:S(2)}, u32[]{:S(2)}) collective-permute-start(f32[6,8,128]{2,1,0:T(8,128)} %get-tuple-element.127.is_ref), channel_id=1, source_target_pairs={{8,0},{9,1},{10,2},{11,3},{12,4},{13,5},{14,6},{15,7},{24,16},{25,... | collective-permute-start | bytes 73736 | tf_op jit(solution)/shard_map/ppermute | solution.py:99
  183.0 5.7 %copy-start.16 = (f32[6,8,128]{2,1,0:T(8,128)}, f32[6,8,128]{2,1,0:T(8,128)S(1)}, u32[]{:S(2)}) copy-start(f32[6,8,128]{2,1,0:T(8,128)S(1)} %collective-permute-done.18.left_ref) | copy-start | bytes 73732
  188.7 0.6 copy-start.20

commit v3 on v1

--- a/solution.py
+++ b/solution.py
@@ -2,10 +2,10 @@
 import jax.numpy as jnp
 from jax import lax
 from jax.experimental import pallas as pl
-from jax.sharding import PartitionSpec as P
+from jax.sharding import Mesh, PartitionSpec as P
 
 
-def local_kernel(f_ref, k_ref, r_ref, a_ref, b_ref, c_ref):
+def local_kernel(f_ref, k_ref, r_ref, a_ref, b_ref, c_ref, e_ref):
     n = f_ref.shape[0]
     zero = jnp.zeros(f_ref.shape[1:], f_ref.dtype)
     ratio, shifted, shifted_b = zero, zero, zero
@@ -30,11 +30,14 @@
         a_ref[i] = later_a
         b_ref[i] = later_b
         c_ref[i] = later_c
+    for j, (ref, at) in enumerate(((a_ref, 0), (b_ref, 0), (c_ref, 0), (a_ref, n - 1), (b_ref, n - 1), (c_ref, n - 1))):
+        e_ref[j] = ref[at]
 
 
 def local_solve(f, k, r):
     shape = jax.ShapeDtypeStruct(f.shape, f.dtype)
-    return pl.pallas_call(local_kernel, out_shape=(shape, shape, shape))(f, k, r)
+    ends = jax.ShapeDtypeStruct((6,) + f.shape[1:], f.dtype)
+    return pl.pallas_call(local_kernel, out_shape=(shape, shape, shape, ends))(f, k, r)
 
 
 def reduced_kernel(coef_ref, out_ref):
@@ -81,10 +84,10 @@
 def solve_along_0(f, k, r, axis):
     count = lax.axis_size(axis)
     n, rows, lanes = f.shape
-    a, b, c = local_solve(f, k, r)
+    a, b, c, coef = local_solve(f, k, r)
     lines = rows * lanes
     m = lines // count
-    coef = jnp.stack([a[0], b[0], c[0], a[n - 1], b[n - 1], c[n - 1]]).reshape(6, count, m)
+    coef = coef.reshape(6, count, m)
     coef = jnp.transpose(coef, (1, 0, 2))
     gathered = lax.all_to_all(coef, axis, 0, 0, tiled=True)
     ends = reduced_solve(gathered)
@@ -93,19 +96,29 @@
     return a + b * ends[0][None] + c * ends[1][None]
 
 
+GROUP = 8
+
+
 def per_device(source, coupling_x, coupling_y, reaction):
-    halfway = solve_along_0(source, coupling_x, reaction, "gx")
+    fields = jnp.stack([source, coupling_x, coupling_y, reaction])
+    fields = lax.all_to_all(fields, "gxi", 3, 1, tiled=True)
+    source, coupling_x, coupling_y, reaction = (fields[i] for i in range(4))
+    halfway = solve_along_0(source, coupling_x, reaction, "gxo")
     turned = solve_along_0(
         jnp.swapaxes(halfway, 0, 1),
         jnp.swapaxes(coupling_y, 0, 1),
         jnp.swapaxes(reaction, 0, 1),
         "gy",
     )
-    return jnp.swapaxes(turned, 0, 1)
+    advanced = jnp.swapaxes(turned, 0, 1)
+    return lax.all_to_all(advanced, "gxi", 0, 2, tiled=True)
 
 
 def solution(mesh):
-    placed = (P("gx", "gy", None), P("gx", "gy", None), P("gx", "gy", None), P("gx", "gy", None))
+    across, down = mesh.shape["gx"], mesh.shape["gy"]
+    inner = GROUP if across % GROUP == 0 else 1
+    grouped = Mesh(mesh.devices.reshape(across // inner, inner, down), ("gxo", "gxi", "gy"))
+    placed = P(("gxo", "gxi"), "gy", None)
     return jax.shard_map(
-        per_device, mesh=mesh, in_specs=placed, out_specs=P("gx", "gy", None), check_vma=False
+        per_device, mesh=grouped, in_specs=(placed,) * 4, out_specs=placed, check_vma=False
     )

time: 136 us -> 162 us (1.19)
  the two profiles are of different devices: /device:TPU:2 before, /device:TPU:1 now
where the time goes in v3:
time: 162 us; the launch traced here: 161 us
  blocking collectives  122 us (75%)
  local copies, waits for them, and re-layouts  19.5 us (12%)
  other arithmetic  9.92 us (6%)
  Pallas kernels  9.31 us (6%)
    all_to_all x2, blocking collectives, solve_along_0(): gathered = lax.all_to_all(coef, axis, 0, 0, tiled=True)  49.8 us
    all_to_all x2, blocking collectives, solve_along_0(): ends = lax.all_to_all(ends, axis, 0, 0, tiled=True)  33.4 us
    all_to_all x1, blocking collectives, per_device(): fields = lax.all_to_all(fields, 'gxi', 3, 1, tiled=True)  25.2 us
    all_to_all x1, blocking collectives, per_device(): return lax.all_to_all(advanced, 'gxi', 0, 2, tiled=True)  14 us
    pallas_call x2, Pallas kernels, local_solve(): pl.pallas_call(local_kernel, out_shape=(shape, shape, shape, ends))(f, k, r)  6.09 us
    unnamed x10, local copies, waits for them, and re-layouts  5.71 us
    all_to_all x2, local copies, waits for them, and re-layouts, per_device(): fields = lax.all_to_all(fields, 'gxi', 3, 1, tiled=True)  3.68 us

profile of v3, /device:TPU:1, one launch (start us, length us, event | category | flops | bytes accessed | tf_op | source)
XLA Modules:
  0.0 161.2 jit_solution(9025966345128315938)
XLA Ops:
  0.0 1.0 pad_maximum_fusion
  1.0 1.8 %copy.50 = f32[4,8,16,128]{2,1,0,3:T(8,128)S(1)} copy(f32[4,8,16,128]{3,2,1,0:T(8,128)S(1)} %pad_maximum_fusion) | data formatting | bytes 524288 | tf_op jit(solution)/shard_map/stack | solution.py:103
  2.8 0.8 reshape.48
  3.5 25.2 %all_to_all.53 = f32[8,1,8192]{2,1,0:T(1,128)S(1)} all-to-all(f32[8,1,8192]{2,1,0:T(1,128)S(1)} %reshape.48), channel_id=1, replica_groups=mesh['gxo'=8,'gxi'=8,'gy'=16] {'gxi'}, dimensions={0} | all-to-all | bytes 524288 | tf_op jit(solution)/shard_map/all_to_all | solution.py:104
  28.7 0.5 broadcast.12
  29.3 1.2 reduce.16
  30.5 2.1 %reshape.49 = f32[128,4,8,16]{3,2,1,0:T(8,128)} reshape(f32[8,8192]{1,0:T(8,128)S(1)} %reduce.16) | data formatting | bytes 524288
  32.6 3.2 %copy.51 = f32[4,8,16,8,16]{4,1,3,2,0:T(8,128)S(1)} copy(f32[4,8,16,8,16]{2,1,0,4,3:T(8,128)} %bitcast.38) | data formatting | bytes 524288 | tf_op jit(solution)/shard_map/all_to_all | solution.py:104
  35.7 1.2 slice_bitcast_fusion.1
  36.9 1.1 copy.54.r_ref
  38.1 1.1 copy.53
  39.2 1.1 copy.52
  40.3 3.3 %shard_map.46 = (f32[64,16,16]{2,1,0:T(8,128)}, f32[64,16,16]{2,1,0:T(8,128)}, f32[64,16,16]{2,1,0:T(8,128)}, f32[6,16,16]{2,1,0:T(8,128)}) custom-call(f32[64,16,16]{2,1,0:T(8,128)} %bitcast.40, f32[64,16,16]{2,1,0:T(8,128)} %bitcast.39, f32[64,16,16]{2,1,0:T(8,128)} %copy.54.r_ref), custom_call_target="tpu_custom_call" | custom-call | tf_op jit(solution)/shard_map/pallas_call | solution.py:40
  43.6 0.9 reshape.24
  44.4 0.1 reshape.50
  44.5 36.8 %all_to_all.54 = f32[8,1,192]{2,1,0:T(1,128)S(1)} all-to-all(f32[8,1,192]{2,1,0:T(1,128)S(1)} %reshape.50), channel_id=1, replica_groups=mesh['gxo'=8,'gxi'=8,'gy'=16] {'gxo'}, dimensions={0} | all-to-all | bytes 12288 | tf_op jit(solution)/shard_map/all_to_all | solution.py:92
  81.4 0.6 reduce.17
  82.0 0.7 reshape.51.coef_ref
  82.7 1.5 shard_map.47
  84.2 24.2 %all_to_all.55 = f32[8,2,32]{2,1,0:T(2,128)S(1)} all-to-all(f32[8,2,32]{2,1,0:T(2,128)} %shard_map.47), channel_id=1, replica_groups=mesh['gxo'=8,'gxi'=8,'gy'=16] {'gxo'}, dimensions={0} | all-to-all | bytes 4096 | tf_op jit(solution)/shard_map/all_to_all | solution.py:94
  108.4 0.1 mul.43
  108.5 0.1 mul.40
  108.6 1.1 broadcast_multiply_fusion
  109.6 2.4 %fusion.1.f_ref = f32[16,64,16]{2,1,0:T(8,128)} fusion(f32[64,16,16]{2,1,0:T(8,128)} %get-tuple-element.16, f32[64,16,16]{2,1,0:T(8,128)S(1)} %broadcast_multiply_fusion, f32[64,16,16]{2,1,0:T(8,128)} %get-tuple-element.13, f32[16,16]{1,0:T(8,128)S(1)} %mul.43), kind=kLoop, calls=%fused_computation.3 | loop fusion | flops 49152 | bytes 263168 | tf_op jit(solution)/shard_map/transpose | solution.py:108
  112.1 2.8 %shard_map.48 = (f32[16,64,16]{2,1,0:T(8,128)}, f32[16,64,16]{2,1,0:T(8,128)}, f32[16,64,16]{2,1,0:T(8,128)}, f32[6,64,16]{2,1,0:T(8,128)}) custom-call(f32[16,64,16]{2,1,0:T(8,128)} %fusion.1.f_ref, f32[16,64,16]{2,1,0:T(8,128)} %get-tuple-element.26.k_ref, f32[16,64,16]{2,1,0:T(8,128)} %get-tuple-element.25.r_ref), custom_call_target="tpu_custom_call" | custom-call | tf_op jit(solution)/shard_map/pallas_call | solution.py:40
  114.9 1.0 reshape.25
  116.0 0.1 reshape.52
  116.1 13.0 %all_to_all.56 = f32[16,1,384]{2,1,0:T(1,128)S(1)} all-to-all(f32[16,1,384]{2,1,0:T(1,128)S(1)} %reshape.52), channel_id=1, replica_groups=mesh['gxo'=8,'gxi'=8,'gy'=16] {'gy'}, dimensions={0} | all-to-all | bytes 49152 | tf_op jit(solution)/shard_map/all_to_all | solution.py:92
  129.1 0.7 reduce.18
  129.7 0.7 reshape.53.coef_ref
  130.4 1.7 %shard_map.49 = f32[16,2,64]{2,1,0:T(2,128)} custom-call(f32[16,6,64]{2,1,0:T(8,128)} %reshape.53.coef_ref), custom_call_target="tpu_custom_call" | custom-call | tf_op jit(solution)/shard_map/pallas_call | solution.py:79
  132.2 0.8 reshape.54
  133.0 9.2 %all_to_all.57 = f32[16,1,128]{2,1,0:T(1,128)S(1)} all-to-all(f32[16,1,128]{2,1,0:T(1,128)S(1)} %reshape.54), channel_id=1, replica_groups=mesh['gxo'=8,'gxi'=8,'gy'=16] {'gy'}, dimensions={0} | all-to-all | bytes 16384 | tf_op jit(solution)/shard_map/all_to_all | solution.py:94
  142.2 0.6 reduce.19
  142.8 0.1 reshape.55
  142.9 0.1 mul.46
  143.0 0.1 mul.49
  143.1 1.5 add_bitcast_fusion
  144.6 0.3 copy.60
  144.9 0.2 reshape.56
  145.1 14.0 %all_to_all.58 = f32[8,1,2048]{2,1,0:T(1,128)S(1)} all-to-all(f32[8,1,2048]{2,1,0:T(1,128)S(1)} %reshape.56), channel_id=1, replica_groups=mesh['gxo'=8,'gxi'=8,'gy'=16] {'gxi'}, dimensions={0} | all-to-all | bytes 131072 | tf_op jit(solution)/shard_map/all_to_all | solution.py:114
  159.1 0.8 reduce.20
  159.9 0.2 reshape.57
  160.1 0.3 copy.61
  160.4 0.8 all_to_all.46
  (4 shorter events, 0.1 us)

commit v4 on v3

--- a/solution.py
+++ b/solution.py
@@ -99,11 +99,55 @@
 GROUP = 8
 
 
+def gathered_kernel(coef_ref, out_ref):
+    count = coef_ref.shape[0]
+    gains = []
+    p_prev = None
+    q_prev = None
+    for d in range(count):
+        a0, b0, c0, a1, b1, c1 = (coef_ref[d, j] for j in range(6))
+        if d == 0:
+            g, h = a0, c0
+            p, q = a1, c1
+        else:
+            denom = 1.0 - b0 * q_prev
+            g = (a0 + b0 * p_prev) / denom
+            h = c0 / denom
+            p = a1 + b1 * p_prev + b1 * q_prev * g
+            q = c1 + b1 * q_prev * h
+        gains.append((g, h, p, q))
+        p_prev, q_prev = p, q
+    later = jnp.zeros_like(gains[0][0])
+    for d in range(count - 1, -1, -1):
+        g, h, _, _ = gains[d]
+        first = g + h * later
+        if d > 0:
+            _, _, p, q = gains[d - 1]
+            before = p + q * first
+        else:
+            before = jnp.zeros_like(first)
+        out_ref[d, 0] = before
+        out_ref[d, 1] = later
+        later = first
+
+
+def solve_gathered(f, k, r, axis):
+    a, b, c, coef = local_solve(f, k, r)
+    everything = lax.all_gather(coef, axis)
+    count = everything.shape[0]
+    ends = pl.pallas_call(
+        gathered_kernel,
+        out_shape=jax.ShapeDtypeStruct((count, 2) + coef.shape[1:], coef.dtype),
+    )(everything)
+    mine = lax.dynamic_index_in_dim(ends, lax.axis_index(axis), 0, keepdims=False)
+    return a + b * mine[0][None] + c * mine[1][None]
+
+
 def per_device(source, coupling_x, coupling_y, reaction):
     fields = jnp.stack([source, coupling_x, coupling_y, reaction])
     fields = lax.all_to_all(fields, "gxi", 3, 1, tiled=True)
     source, coupling_x, coupling_y, reaction = (fields[i] for i in range(4))
-    halfway = solve_along_0(source, coupling_x, reaction, "gxo")
+    halfway = solve_gathered(source, coupling_x, reaction, "gxo")
     turned = solve_along_0(
         jnp.swapaxes(halfway, 0, 1),
         jnp.swapaxes(coupling_y, 0, 1),

time: 162 us -> 142 us (0.88)
  blocking collectives: 122 us -> 78 us
  starting transfers between devices: 0 us -> 17.4 us
  waiting for transfers between devices: 0 us -> 8.7 us
  other arithmetic: 9.92 us -> 8.09 us
    all_gather x0 -> x1, blocking collectives: none -> 39 us  [solve_gathered(): everything = lax.all_gather(coef, axis)]
    all_to_all x2 -> x1, blocking collectives: 49.8 us -> 13 us  [solve_along_0(): gathered = lax.all_to_all(coef, axis, 0, 0, tiled=True)]
    all_to_all x1 -> x0, blocking collectives: 25.2 us -> none  [per_device(): fields = lax.all_to_all(fields, 'gxi', 3, 1, tiled=True)]
    all_to_all x2 -> x1, blocking collectives: 33.4 us -> 9.18 us  [solve_along_0(): ends = lax.all_to_all(ends, axis, 0, 0, tiled=True)]
    all_to_all x0 -> x1, starting transfers between devices: none -> 17.4 us  [per_device(): fields = lax.all_to_all(fields, 'gxi', 3, 1, tiled=True)]
    all_to_all x0 -> x1, waiting for transfers between devices: none -> 8.7 us  [per_device(): fields = lax.all_to_all(fields, 'gxi', 3, 1, tiled=True)]
    all_to_all x1, blocking collectives: 14 us -> 16.8 us  [per_device(): return lax.all_to_all(advanced, 'gxi', 0, 2, tiled=True)]
    pallas_call x0 -> x1, Pallas kernels: none -> 1.75 us  [solve_gathered(): pl.pallas_call(gathered_kernel, out_shape=jax.ShapeDtypeStruct((count, 2)...]
  transfers between devices with their start and end apart: 0 -> 1, of which waited for: 0 -> 1; matrix products, arithmetic and copies ran while one was open for 0% -> 0% of each run, Pallas kernels for 0% -> 0%
where the time goes in v4:
time: 142 us; the launch traced here: 141 us
  blocking collectives  78 us (55%)
  local copies, waits for them, and re-layouts  19.1 us (13%)
  starting transfers between devices  17.4 us (12%)
  Pallas kernels  9.55 us (7%)
  waiting for transfers between devices  8.7 us (6%)
  other arithmetic  8.09 us (6%)
    all_gather x1, blocking collectives, solve_gathered(): everything = lax.all_gather(coef, axis)  39 us
    all_to_all x1, starting transfers between devices, per_device(): fields = lax.all_to_all(fields, 'gxi', 3, 1, tiled=True)  17.4 us
    all_to_all x1, blocking collectives, per_device(): return lax.all_to_all(advanced, 'gxi', 0, 2, tiled=True)  16.8 us
    all_to_all x1, blocking collectives, solve_along_0(): gathered = lax.all_to_all(coef, axis, 0, 0, tiled=True)  13 us
    all_to_all x1, blocking collectives, solve_along_0(): ends = lax.all_to_all(ends, axis, 0, 0, tiled=True)  9.18 us
    all_to_all x1, waiting for transfers between devices, per_device(): fields = lax.all_to_all(fields, 'gxi', 3, 1, tiled=True)  8.7 us
    pallas_call x2, Pallas kernels, local_solve(): pl.pallas_call(local_kernel, out_shape=(shape, shape, shape, ends))(f, k, r)  6.07 us
    unnamed x12, local copies, waits for them, and re-layouts  5.64 us
  transfers between devices with their start and end apart: 1, of which 1 were waited for; matrix products, arithmetic and copies ran while one was open for 0% of the time, Pallas kernels for 0%

profile of v4, /device:TPU:1, one launch (start us, length us, event | category | flops | bytes accessed | tf_op | source)
XLA Modules:
  0.0 141.0 jit_solution(14517177295651360915)
XLA Ops:
  0.0 1.0 pad_maximum_fusion
  1.0 1.8 %copy.47 = f32[4,8,16,128]{2,1,0,3:T(8,128)S(1)} copy(f32[4,8,16,128]{3,2,1,0:T(8,128)S(1)} %pad_maximum_fusion) | data formatting | bytes 524288 | tf_op jit(solution)/shard_map/stack | solution.py:147
  2.8 1.4 %reshape.34 = f32[8,1,8192]{2,1,0:T(1,128)} reshape(f32[128,4,8,16]{3,2,1,0:T(8,128)S(1)} %bitcast.37) | data formatting | bytes 524288
  4.2 17.4 %all-to-all-start = ((f32[8,1,8192]{2,1,0:T(1,128)}), f32[8,1,8192]{2,1,0:T(1,128)S(1)}, u32[]{:S(2)}, u32[]{:S(2)}) async-start(f32[8,1,8192]{2,1,0:T(1,128)} %reshape.34), calls=%async_computation | async-start | bytes 524288 | tf_op jit(solution)/shard_map/all_to_all | solution.py:148
  21.7 8.7 %all-to-all-done = f32[8,1,8192]{2,1,0:T(1,128)S(1)} async-done(((f32[8,1,8192]{2,1,0:T(1,128)}), f32[8,1,8192]{2,1,0:T(1,128)S(1)}, u32[]{:S(2)}, u32[]{:S(2)}) %all-to-all-start) | async-done | bytes 262176 | tf_op jit(solution)/shard_map/all_to_all | solution.py:148
  30.4 0.5 broadcast.6
  30.9 1.2 reduce.8
  32.1 2.1 %reshape.35 = f32[128,4,8,16]{3,2,1,0:T(8,128)} reshape(f32[8,8192]{1,0:T(8,128)S(1)} %reduce.8) | data formatting | bytes 524288
  34.2 3.2 %copy.48 = f32[4,8,16,8,16]{4,1,3,2,0:T(8,128)S(1)} copy(f32[4,8,16,8,16]{2,1,0,4,3:T(8,128)} %bitcast.39) | data formatting | bytes 524288 | tf_op jit(solution)/shard_map/all_to_all | solution.py:148
  37.4 1.2 slice_bitcast_fusion.1
  38.6 1.1 copy.49
  39.7 1.1 copy.50
  40.8 1.1 copy.51.r_ref
  41.9 3.3 %shard_map.46 = (f32[64,16,16]{2,1,0:T(8,128)}, f32[64,16,16]{2,1,0:T(8,128)}, f32[64,16,16]{2,1,0:T(8,128)}, f32[6,16,16]{2,1,0:T(8,128)}) custom-call(f32[64,16,16]{2,1,0:T(8,128)} %bitcast.40, f32[64,16,16]{2,1,0:T(8,128)} %bitcast.41, f32[64,16,16]{2,1,0:T(8,128)} %copy.51.r_ref), custom_call_target="tpu_custom_call" | custom-call | tf_op jit(solution)/shard_map/pallas_call | solution.py:40
  45.2 0.0 copy-start
  45.2 0.0 copy-start.1
  45.2 39.0 %all-gather = f32[48,16,16]{2,1,0:T(8,128)} all-gather(f32[6,16,16]{2,1,0:T(8,128)} %get-tuple-element.15), channel_id=2, replica_groups=mesh['gxo'=8,'gxi'=8,'gy'=16] {'gxo'}, dimensions={0}, use_global_device_ids=true | all-gather | bytes 55296 | tf_op jit(solution)/shard_map/all_gather | solution.py:136
  84.2 1.7 %shard_map.47 = f32[8,2,16,16]{3,2,1,0:T(8,128)} custom-call(f32[8,6,16,16]{3,2,1,0:T(8,128)} %bitcast.43), custom_call_target="tpu_custom_call" | custom-call | tf_op jit(solution)/shard_map/pallas_call | solution.py:138
  86.0 0.7 dynamic-slice_bitcast_fusion
  86.7 1.1 broadcast_multiply_fusion
  87.8 0.0 copy-done
  87.8 0.0 copy-done.1
  87.8 1.3 fusion.1.f_ref
  89.0 2.8 %shard_map.48 = (f32[16,64,16]{2,1,0:T(8,128)}, f32[16,64,16]{2,1,0:T(8,128)}, f32[16,64,16]{2,1,0:T(8,128)}, f32[6,64,16]{2,1,0:T(8,128)}) custom-call(f32[16,64,16]{2,1,0:T(8,128)} %fusion.1.f_ref, f32[16,64,16]{2,1,0:T(8,128)} %get-tuple-element.24.k_ref, f32[16,64,16]{2,1,0:T(8,128)} %get-tuple-element.23.r_ref), custom_call_target="tpu_custom_call" | custom-call | tf_op jit(solution)/shard_map/pallas_call | solution.py:40
  91.9 1.0 reshape.20
  92.9 0.1 reshape.36
  93.0 13.0 %all_to_all.43 = f32[16,1,384]{2,1,0:T(1,128)S(1)} all-to-all(f32[16,1,384]{2,1,0:T(1,128)S(1)} %reshape.36), channel_id=1, replica_groups=mesh['gxo'=8,'gxi'=8,'gy'=16] {'gy'}, dimensions={0} | all-to-all | bytes 49152 | tf_op jit(solution)/shard_map/all_to_all | solution.py:92
  106.0 0.7 reduce.9
  106.7 0.7 reshape.37.coef_ref
  107.4 1.7 %shard_map.49 = f32[16,2,64]{2,1,0:T(2,128)} custom-call(f32[16,6,64]{2,1,0:T(8,128)} %reshape.37.coef_ref), custom_call_target="tpu_custom_call" | custom-call | tf_op jit(solution)/shard_map/pallas_call | solution.py:79
  109.1 0.8 reshape.38
  109.9 9.2 %all_to_all.44 = f32[16,1,128]{2,1,0:T(1,128)S(1)} all-to-all(f32[16,1,128]{2,1,0:T(1,128)S(1)} %reshape.38), channel_id=1, replica_groups=mesh['gxo'=8,'gxi'=8,'gy'=16] {'gy'}, dimensions={0} | all-to-all | bytes 16384 | tf_op jit(solution)/shard_map/all_to_all | solution.py:94
  119.1 0.6 reduce.10
  119.8 0.1 reshape.39
  119.9 0.1 mul.46
  120.0 0.1 mul.49
  120.0 1.5 %add_bitcast_fusion = f32[64,16,16]{2,0,1:T(8,128)S(1)} fusion(f32[16,64,16]{2,1,0:T(8,128)} %get-tuple-element.20, f32[16,64,16]{2,1,0:T(8,128)} %get-tuple-element.17, f32[16,64,16]{2,1,0:T(8,128)} %get-tuple-element.18, f32[64,16]{1,0:T(8,128)S(1)} %mul.49, f32[64,16]{1,0:T(8,128)S(1)} %mul.46), kind=kLoop, calls=%fused_computation.5 | loop fusion | flops 65536 | bytes 270336 | tf_op jit(solution)/shard_map/transpose | solution.py:157
  121.5 0.3 copy.56
  121.9 0.2 reshape.40
  122.1 16.8 %all_to_all.45 = f32[8,1,2048]{2,1,0:T(1,128)S(1)} all-to-all(f32[8,1,2048]{2,1,0:T(1,128)S(1)} %reshape.40), channel_id=1, replica_groups=mesh['gxo'=8,'gxi'=8,'gy'=16] {'gxi'}, dimensions={0} | all-to-all | bytes 131072 | tf_op jit(solution)/shard_map/all_to_all | solution.py:158
  138.9 0.8 reduce.11
  139.6 0.2 reshape.41
  139.8 0.3 copy.57
  140.2 0.8 all_to_all.38
  (2 shorter events, 0.1 us)
Async XLA Ops:
  4.2 26.1 %all-to-all-start = ((f32[8,1,8192]{2,1,0:T(1,128)}), f32[8,1,8192]{2,1,0:T(1,128)S(1)}, u32[]{:S(2)}, u32[]{:S(2)}) async-start(f32[8,1,8192]{2,1,0:T(1,128)} %reshape.34), calls=%async_computation | async-start | bytes 524288 | tf_op jit(solution)/shard_map/all_to_all | solution.py:148
  45.2 42.6 %copy-start = (f32[64,16,16]{2,1,0:T(8,128)S(1)}, f32[64,16,16]{2,1,0:T(8,128)}, u32[]{:S(2)}) copy-start(f32[64,16,16]{2,1,0:T(8,128)} %get-tuple-element.13) | copy-start | bytes 196612
  45.2 42.6 %copy-start.1 = (f32[64,16,16]{2,1,0:T(8,128)S(1)}, f32[64,16,16]{2,1,0:T(8,128)}, u32[]{:S(2)}) copy-start(f32[64,16,16]{2,1,0:T(8,128)} %get-tuple-element.16) | copy-start | bytes 196612

commit v5 on v1

--- a/solution.py
+++ b/solution.py
@@ -5,7 +5,7 @@
 from jax.sharding import PartitionSpec as P
 
 
-def local_kernel(f_ref, k_ref, r_ref, a_ref, b_ref, c_ref):
+def local_kernel(f_ref, k_ref, r_ref, a_ref, b_ref, c_ref, e_ref):
     n = f_ref.shape[0]
     zero = jnp.zeros(f_ref.shape[1:], f_ref.dtype)
     ratio, shifted, shifted_b = zero, zero, zero
@@ -30,11 +30,14 @@
         a_ref[i] = later_a
         b_ref[i] = later_b
         c_ref[i] = later_c
+    for j, (ref, at) in enumerate(((a_ref, 0), (b_ref, 0), (c_ref, 0), (a_ref, n - 1), (b_ref, n - 1), (c_ref, n - 1))):
+        e_ref[j] = ref[at]
 
 
 def local_solve(f, k, r):
     shape = jax.ShapeDtypeStruct(f.shape, f.dtype)
-    return pl.pallas_call(local_kernel, out_shape=(shape, shape, shape))(f, k, r)
+    ends = jax.ShapeDtypeStruct((6,) + f.shape[1:], f.dtype)
+    return pl.pallas_call(local_kernel, out_shape=(shape, shape, shape, ends))(f, k, r)
 
 
 def reduced_kernel(coef_ref, out_ref):
@@ -81,10 +84,10 @@
 def solve_along_0(f, k, r, axis):
     count = lax.axis_size(axis)
     n, rows, lanes = f.shape
-    a, b, c = local_solve(f, k, r)
+    a, b, c, coef = local_solve(f, k, r)
     lines = rows * lanes
     m = lines // count
-    coef = jnp.stack([a[0], b[0], c[0], a[n - 1], b[n - 1], c[n - 1]]).reshape(6, count, m)
+    coef = coef.reshape(6, count, m)
     coef = jnp.transpose(coef, (1, 0, 2))
     gathered = lax.all_to_all(coef, axis, 0, 0, tiled=True)
     ends = reduced_solve(gathered)

time: 136 us -> 130 us (0.956)
  local copies, waits for them, and re-layouts: 13.8 us -> 7.65 us
    unnamed x32 -> x22, local copies, waits for them, and re-layouts: 9.62 us -> 3.4 us
    reshape x4, local copies, waits for them, and re-layouts: 0.32 us -> 1.84 us  [solve_along_0(): coef = coef.reshape(6, count, m)]
    another operation x2 -> x0, local copies, waits for them, and re-layouts: 1.38 us -> none  [solve_along_0(): jnp.stack([a[0], b[0], c[0], a[n - 1], b[n - 1], c[n - 1]])]
where the time goes in v5:
time: 130 us; the launch traced here: 129 us
  blocking collectives  79.8 us (61%)
  waiting for transfers between devices  25.7 us (20%)
  Pallas kernels  8.04 us (6%)
  local copies, waits for them, and re-layouts  7.65 us (6%)
  starting transfers between devices  4.73 us (4%)
  other arithmetic  2.96 us (2%)
    all_to_all x2, blocking collectives, solve_along_0(): gathered = lax.all_to_all(coef, axis, 0, 0, tiled=True)  69 us
    all_to_all x1, waiting for transfers between devices, solve_along_0(): ends = lax.all_to_all(ends, axis, 0, 0, tiled=True)  25.7 us
    all_to_all x1, blocking collectives, solve_along_0(): ends = lax.all_to_all(ends, axis, 0, 0, tiled=True)  10.8 us
    all_to_all x1, starting transfers between devices, solve_along_0(): ends = lax.all_to_all(ends, axis, 0, 0, tiled=True)  4.73 us
    pallas_call x2, Pallas kernels, reduced_solve(): pl.pallas_call(reduced_kernel, out_shape=jax.ShapeDtypeStruct((count, 2,...  4.59 us
    pallas_call x2, Pallas kernels, local_solve(): pl.pallas_call(local_kernel, out_shape=(shape, shape, shape, ends))(f, k, r)  3.45 us
    unnamed x22, local copies, waits for them, and re-layouts  3.4 us
  transfers between devices with their start and end apart: 1, of which 1 were waited for; matrix products, arithmetic and copies ran while one was open for 1% of the time, Pallas kernels for 0%

profile of v5, /device:TPU:2, one launch (start us, length us, event | category | flops | bytes accessed | tf_op | source)
XLA Modules:
  0.0 128.9 jit_solution(8043969573615480229)
XLA Ops:
  0.0 1.7 %shard_map.46 = (f32[8,16,128]{2,1,0:T(8,128)}, f32[8,16,128]{2,1,0:T(8,128)}, f32[8,16,128]{2,1,0:T(8,128)}, f32[6,16,128]{2,1,0:T(8,128)}) custom-call(f32[8,16,128]{2,1,0:T(8,128)} %f_ref.1, f32[8,16,128]{2,1,0:T(8,128)} %k_ref.1, f32[8,16,128]{2,1,0:T(8,128)} %r_ref.1), custom_call_target="tpu_custom_call" | custom-call | tf_op jit(solution)/shard_map/pallas_call | solution.py:40
  1.7 0.9 reshape.16
  2.6 0.1 copy.34
  2.7 0.2 reshape.40
  2.9 55.5 %all_to_all.20 = f32[64,1,192]{2,1,0:T(1,128)S(1)} all-to-all(f32[64,1,192]{2,1,0:T(1,128)S(1)} %reshape.40), channel_id=1, replica_groups=mesh['gx'=64,'gy'=16] {'gx'}, dimensions={0} | all-to-all | bytes 98304 | tf_op jit(solution)/shard_map/all_to_all | solution.py:92
  58.4 0.6 broadcast.12
  59.0 0.8 reduce.16
  59.8 0.8 reshape.41.coef_ref
  60.6 2.8 %shard_map.47 = f32[64,2,32]{2,1,0:T(2,128)} custom-call(f32[64,6,32]{2,1,0:T(8,128)} %reshape.41.coef_ref), custom_call_target="tpu_custom_call" | custom-call | tf_op jit(solution)/shard_map/pallas_call | solution.py:79
  63.4 0.0 copy-start
  63.4 0.0 copy-start.4
  63.4 4.7 %all-to-all-start.1 = ((f32[64,2,32]{2,1,0:T(2,128)}), f32[64,2,32]{2,1,0:T(2,128)S(1)}, u32[]{:S(2)}, u32[]{:S(2)}) async-start(f32[64,2,32]{2,1,0:T(2,128)} %shard_map.47), calls=%async_computation.1 | async-start | bytes 131072 | tf_op jit(solution)/shard_map/all_to_all | solution.py:94
  68.2 0.0 copy-done
  68.2 0.0 copy-done.4
  68.2 0.7 copy_bitcast_fusion.2
  68.9 25.7 %all-to-all-done.1 = f32[64,2,32]{2,1,0:T(2,128)S(1)} async-done(((f32[64,2,32]{2,1,0:T(2,128)}), f32[64,2,32]{2,1,0:T(2,128)S(1)}, u32[]{:S(2)}, u32[]{:S(2)}) %all-to-all-start.1) | async-done | bytes 16416 | tf_op jit(solution)/shard_map/all_to_all | solution.py:94
  94.5 0.0 copy-start.2
  94.5 0.0 copy-start.3
  94.5 0.2 slice_reduce_fusion.1
  94.7 0.0 copy-start.1
  94.7 0.1 mul.43
  94.8 0.1 mul.40
  94.9 0.5 copy-done.2
  95.4 0.0 copy-done.3
  95.4 0.2 copy-done.1
  95.6 0.7 fusion.1.f_ref
  96.3 1.8 %shard_map.48 = (f32[16,8,128]{2,1,0:T(8,128)}, f32[16,8,128]{2,1,0:T(8,128)}, f32[16,8,128]{2,1,0:T(8,128)}, f32[6,8,128]{2,1,0:T(8,128)}) custom-call(f32[16,8,128]{2,1,0:T(8,128)} %fusion.1.f_ref, f32[16,8,128]{2,1,0:T(8,128)} %get-tuple-element.26.k_ref, f32[16,8,128]{2,1,0:T(8,128)} %get-tuple-element.25.r_ref), custom_call_target="tpu_custom_call" | custom-call | tf_op jit(solution)/shard_map/pallas_call | solution.py:40
  98.1 0.8 reshape.17
  98.9 0.1 reshape.42
  99.0 13.5 %all_to_all.21 = f32[16,1,384]{2,1,0:T(1,128)S(1)} all-to-all(f32[16,1,384]{2,1,0:T(1,128)S(1)} %reshape.42), channel_id=1, replica_groups=mesh['gx'=64,'gy'=16] {'gy'}, dimensions={0} | all-to-all | bytes 49152 | tf_op jit(solution)/shard_map/all_to_all | solution.py:92
  112.5 0.7 reduce.17
  113.2 0.7 reshape.43.coef_ref
  113.9 0.0 copy-start.7
  113.9 1.8 %shard_map.49 = f32[16,2,64]{2,1,0:T(2,128)} custom-call(f32[16,6,64]{2,1,0:T(8,128)} %reshape.43.coef_ref), custom_call_target="tpu_custom_call" | custom-call | tf_op jit(solution)/shard_map/pallas_call | solution.py:79
  115.7 0.0 copy-start.6
  115.7 0.8 reshape.44
  116.5 0.0 copy-start.5
  116.5 10.8 %all_to_all.22 = f32[16,1,128]{2,1,0:T(1,128)S(1)} all-to-all(f32[16,1,128]{2,1,0:T(1,128)S(1)} %reshape.44), channel_id=1, replica_groups=mesh['gx'=64,'gy'=16] {'gy'}, dimensions={0} | all-to-all | bytes 16384 | tf_op jit(solution)/shard_map/all_to_all | solution.py:94
  127.3 0.7 reduce.18
  128.0 0.1 reshape.45
  128.1 0.1 mul.49
  128.2 0.1 mul.46
  128.3 0.0 copy-done.7
  128.3 0.0 copy-done.6
  128.3 0.0 copy-done.5
  128.3 0.6 copy.18
  (3 shorter events, 0.1 us)
Async XLA Ops:
  63.4 4.7 %copy-start = (f32[8,16,128]{2,1,0:T(8,128)S(1)}, f32[8,16,128]{2,1,0:T(8,128)}, u32[]{:S(2)}) copy-start(f32[8,16,128]{2,1,0:T(8,128)} %r_ref.1) | copy-start | bytes 196612
  63.4 4.8 %copy-start.4 = (f32[8,16,128]{2,1,0:T(8,128)S(1)}, f32[8,16,128]{2,1,0:T(8,128)}, u32[]{:S(2)}) copy-start(f32[8,16,128]{2,1,0:T(8,128)} %param.6) | copy-start | bytes 196612
  63.4 31.1 %all-to-all-start.1 = ((f32[64,2,32]{2,1,0:T(2,128)}), f32[64,2,32]{2,1,0:T(2,128)S(1)}, u32[]{:S(2)}, u32[]{:S(2)}) async-start(f32[64,2,32]{2,1,0:T(2,128)} %shard_map.47), calls=%async_computation.1 | async-start | bytes 131072 | tf_op jit(solution)/shard_map/all_to_all | solution.py:94
  94.5 0.8 copy-start.2
  94.5 0.9 copy-start.3
  94.7 0.9 copy-start.1
  113.9 14.3 %copy-start.7 = (f32[16,8,128]{2,1,0:T(8,128)S(1)}, f32[16,8,128]{2,1,0:T(8,128)}, u32[]{:S(2)}) copy-start(f32[16,8,128]{2,1,0:T(8,128)} %get-tuple-element.20) | copy-start | bytes 196612
  115.7 12.6 %copy-start.6 = (f32[16,8,128]{2,1,0:T(8,128)S(1)}, f32[16,8,128]{2,1,0:T(8,128)}, u32[]{:S(2)}) copy-start(f32[16,8,128]{2,1,0:T(8,128)} %get-tuple-element.18) | copy-start | bytes 196612
  116.5 11.7 %copy-start.5 = (f32[16,8,128]{2,1,0:T(8,128)S(1)}, f32[16,8,128]{2,1,0:T(8,128)}, u32[]{:S(2)}) copy-start(f32[16,8,128]{2,1,0:T(8,128)} %get-tuple-element.17) | copy-start | bytes 196612

commit v6 on v5

--- a/solution.py
+++ b/solution.py
@@ -45,10 +45,11 @@
     gains = []
     p_prev = None
     q_prev = None
+    m = coef_ref.shape[2] // 6
     for d in range(count):
         row = coef_ref[d]
-        a0, b0, c0 = row[0:1], row[1:2], row[2:3]
-        a1, b1, c1 = row[3:4], row[4:5], row[5:6]
+        a0, b0, c0 = row[:, 0:m], row[:, m:2 * m], row[:, 2 * m:3 * m]
+        a1, b1, c1 = row[:, 3 * m:4 * m], row[:, 4 * m:5 * m], row[:, 5 * m:6 * m]
         if d == 0:
             g, h = a0, c0
             p, q = a1, c1
@@ -75,9 +76,9 @@
 
 
 def reduced_solve(coef):
-    count, _, m = coef.shape
+    count, _, width = coef.shape
     return pl.pallas_call(
-        reduced_kernel, out_shape=jax.ShapeDtypeStruct((count, 2, m), coef.dtype)
+        reduced_kernel, out_shape=jax.ShapeDtypeStruct((count, 2, width // 6), coef.dtype)
     )(coef)
 
 
@@ -88,7 +89,7 @@
     lines = rows * lanes
     m = lines // count
     coef = coef.reshape(6, count, m)
-    coef = jnp.transpose(coef, (1, 0, 2))
+    coef = jnp.transpose(coef, (1, 0, 2)).reshape(count, 1, 6 * m)
     gathered = lax.all_to_all(coef, axis, 0, 0, tiled=True)
     ends = reduced_solve(gathered)
     ends = lax.all_to_all(ends, axis, 0, 0, tiled=True)

time: 130 us -> 150 us (1.15)
  Pallas kernels: 8.04 us -> 30.8 us
  local copies, waits for them, and re-layouts: 7.65 us -> 6.02 us
  other arithmetic: 2.96 us -> 1.37 us
    pallas_call x2, Pallas kernels: 4.59 us -> 27.4 us  [reduced_solve(): pl.pallas_call(reduced_kernel, out_shape=jax.ShapeDtypeStruct((count, 2,...]
    unnamed x22 -> x18, local copies, waits for them, and re-layouts: 3.4 us -> 1.64 us
    all_to_all x2 -> x0, other arithmetic: 1.55 us -> none  [solve_along_0(): gathered = lax.all_to_all(coef, axis, 0, 0, tiled=True)]
  transfers between devices with their start and end apart: 1 -> 1, of which waited for: 1 -> 1; matrix products, arithmetic and copies ran while one was open for 1% -> 0% of each run, Pallas kernels for 0% -> 0%
where the time goes in v6:
time: 150 us; the launch traced here: 149 us
  blocking collectives  80.1 us (53%)
  Pallas kernels  30.8 us (21%)
  waiting for transfers between devices  25.7 us (17%)
  local copies, waits for them, and re-layouts  6.02 us (4%)
  starting transfers between devices  4.74 us (3%)
    all_to_all x2, blocking collectives, solve_along_0(): gathered = lax.all_to_all(coef, axis, 0, 0, tiled=True)  69.4 us
    pallas_call x2, Pallas kernels, reduced_solve(): pl.pallas_call(reduced_kernel, out_shape=jax.ShapeDtypeStruct((count, 2,...  27.4 us
    all_to_all x1, waiting for transfers between devices, solve_along_0(): ends = lax.all_to_all(ends, axis, 0, 0, tiled=True)  25.7 us
    all_to_all x1, blocking collectives, solve_along_0(): ends = lax.all_to_all(ends, axis, 0, 0, tiled=True)  10.8 us
    all_to_all x1, starting transfers between devices, solve_along_0(): ends = lax.all_to_all(ends, axis, 0, 0, tiled=True)  4.74 us
    pallas_call x2, Pallas kernels, local_solve(): pl.pallas_call(local_kernel, out_shape=(shape, shape, shape, ends))(f, k, r)  3.43 us
  transfers between devices with their start and end apart: 1, of which 1 were waited for; matrix products, arithmetic and copies ran while one was open for 0% of the time, Pallas kernels for 0%

profile of v6, /device:TPU:2, one launch (start us, length us, event | category | flops | bytes accessed | tf_op | source)
XLA Modules:
  0.0 148.8 jit_solution(13545498161493447872)
XLA Ops:
  0.0 1.7 %shard_map.46 = (f32[8,16,128]{2,1,0:T(8,128)}, f32[8,16,128]{2,1,0:T(8,128)}, f32[8,16,128]{2,1,0:T(8,128)}, f32[6,16,128]{2,1,0:T(8,128)}) custom-call(f32[8,16,128]{2,1,0:T(8,128)} %f_ref.1, f32[8,16,128]{2,1,0:T(8,128)} %k_ref.1, f32[8,16,128]{2,1,0:T(8,128)} %r_ref.1), custom_call_target="tpu_custom_call" | custom-call | tf_op jit(solution)/shard_map/pallas_call | solution.py:40
  1.7 0.9 reshape.22
  2.6 0.1 copy.13
  2.7 0.1 copy.14
  2.8 55.6 %all_to_all.20.coef_ref = f32[64,1,192]{2,1,0:T(1,128)} all-to-all(f32[64,1,192]{2,1,0:T(1,128)S(1)} %copy.14), channel_id=1, replica_groups=mesh['gx'=64,'gy'=16] {'gx'}, dimensions={0} | all-to-all | bytes 98304 | tf_op jit(solution)/shard_map/all_to_all | solution.py:93
  58.4 23.8 %shard_map.47 = f32[64,2,32]{2,1,0:T(2,128)} custom-call(f32[64,1,192]{2,1,0:T(1,128)} %all_to_all.20.coef_ref), custom_call_target="tpu_custom_call" | custom-call | tf_op jit(solution)/shard_map/pallas_call | solution.py:80
  82.2 0.0 copy-start
  82.2 0.0 copy-start.4
  82.2 4.7 %all-to-all-start.1 = ((f32[64,2,32]{2,1,0:T(2,128)}), f32[64,2,32]{2,1,0:T(2,128)S(1)}, u32[]{:S(2)}, u32[]{:S(2)}) async-start(f32[64,2,32]{2,1,0:T(2,128)} %shard_map.47), calls=%async_computation.1 | async-start | bytes 131072 | tf_op jit(solution)/shard_map/all_to_all | solution.py:95
  87.0 0.0 copy-done
  87.0 0.0 copy-done.4
  87.0 0.7 copy_bitcast_fusion.1
  87.7 25.7 %all-to-all-done.1 = f32[64,2,32]{2,1,0:T(2,128)S(1)} async-done(((f32[64,2,32]{2,1,0:T(2,128)}), f32[64,2,32]{2,1,0:T(2,128)S(1)}, u32[]{:S(2)}, u32[]{:S(2)}) %all-to-all-start.1) | async-done | bytes 16416 | tf_op jit(solution)/shard_map/all_to_all | solution.py:95
  113.3 0.0 copy-start.2
  113.3 0.0 copy-start.3
  113.3 0.2 slice_reduce_fusion.1
  113.5 0.0 copy-start.1
  113.5 0.1 mul.43
  113.6 0.1 mul.40
  113.7 0.5 copy-done.2
  114.2 0.0 copy-done.3
  114.2 0.2 copy-done.1
  114.4 0.7 fusion.1.f_ref
  115.1 1.8 %shard_map.48 = (f32[16,8,128]{2,1,0:T(8,128)}, f32[16,8,128]{2,1,0:T(8,128)}, f32[16,8,128]{2,1,0:T(8,128)}, f32[6,8,128]{2,1,0:T(8,128)}) custom-call(f32[16,8,128]{2,1,0:T(8,128)} %fusion.1.f_ref, f32[16,8,128]{2,1,0:T(8,128)} %get-tuple-element.26.k_ref, f32[16,8,128]{2,1,0:T(8,128)} %get-tuple-element.25.r_ref), custom_call_target="tpu_custom_call" | custom-call | tf_op jit(solution)/shard_map/pallas_call | solution.py:40
  116.8 0.8 reshape.24
  117.7 0.1 reshape.26
  117.8 0.0 copy-start.7
  117.8 13.7 %all_to_all.21.coef_ref = f32[16,1,384]{2,1,0:T(1,128)} all-to-all(f32[16,1,384]{2,1,0:T(1,128)S(1)} %reshape.26), channel_id=1, replica_groups=mesh['gx'=64,'gy'=16] {'gy'}, dimensions={0} | all-to-all | bytes 49152 | tf_op jit(solution)/shard_map/all_to_all | solution.py:93
  131.5 3.6 %shard_map.49 = f32[16,2,64]{2,1,0:T(2,128)} custom-call(f32[16,1,384]{2,1,0:T(1,128)} %all_to_all.21.coef_ref), custom_call_target="tpu_custom_call" | custom-call | tf_op jit(solution)/shard_map/pallas_call | solution.py:80
  135.1 0.0 copy-start.6
  135.1 0.8 reshape.49
  135.9 0.0 copy-start.5
  135.9 10.8 %all_to_all.22 = f32[16,1,128]{2,1,0:T(1,128)S(1)} all-to-all(f32[16,1,128]{2,1,0:T(1,128)S(1)} %reshape.49), channel_id=1, replica_groups=mesh['gx'=64,'gy'=16] {'gy'}, dimensions={0} | all-to-all | bytes 16384 | tf_op jit(solution)/shard_map/all_to_all | solution.py:95
  146.7 0.5 broadcast.12
  147.2 0.7 reduce.16
  147.9 0.1 reshape.50
  148.0 0.1 mul.49
  148.1 0.1 mul.46
  148.1 0.0 copy-done.7
  148.1 0.0 copy-done.6
  148.1 0.0 copy-done.5
  148.2 0.6 copy.22
  (3 shorter events, 0.1 us)
Async XLA Ops:
  82.2 4.8 %copy-start = (f32[8,16,128]{2,1,0:T(8,128)S(1)}, f32[8,16,128]{2,1,0:T(8,128)}, u32[]{:S(2)}) copy-start(f32[8,16,128]{2,1,0:T(8,128)} %r_ref.1) | copy-start | bytes 196612
  82.2 4.8 %copy-start.4 = (f32[8,16,128]{2,1,0:T(8,128)S(1)}, f32[8,16,128]{2,1,0:T(8,128)}, u32[]{:S(2)}) copy-start(f32[8,16,128]{2,1,0:T(8,128)} %param.6) | copy-start | bytes 196612
  82.2 31.1 %all-to-all-start.1 = ((f32[64,2,32]{2,1,0:T(2,128)}), f32[64,2,32]{2,1,0:T(2,128)S(1)}, u32[]{:S(2)}, u32[]{:S(2)}) async-start(f32[64,2,32]{2,1,0:T(2,128)} %shard_map.47), calls=%async_computation.1 | async-start | bytes 131072 | tf_op jit(solution)/shard_map/all_to_all | solution.py:95
  113.3 0.8 copy-start.2
  113.3 0.9 copy-start.3
  113.5 0.9 copy-start.1
  117.8 30.4 %copy-start.7 = (f32[16,8,128]{2,1,0:T(8,128)S(1)}, f32[16,8,128]{2,1,0:T(8,128)}, u32[]{:S(2)}) copy-start(f32[16,8,128]{2,1,0:T(8,128)} %get-tuple-element.20) | copy-start | bytes 196612
  135.1 13.1 %copy-start.6 = (f32[16,8,128]{2,1,0:T(8,128)S(1)}, f32[16,8,128]{2,1,0:T(8,128)}, u32[]{:S(2)}) copy-start(f32[16,8,128]{2,1,0:T(8,128)} %get-tuple-element.18) | copy-start | bytes 196612
  135.9 12.2 %copy-start.5 = (f32[16,8,128]{2,1,0:T(8,128)S(1)}, f32[16,8,128]{2,1,0:T(8,128)}, u32[]{:S(2)}) copy-start(f32[16,8,128]{2,1,0:T(8,128)} %get-tuple-element.17) | copy-start | bytes 196612

commit v7 on v6

--- a/solution.py
+++ b/solution.py
@@ -46,10 +46,10 @@
     p_prev = None
     q_prev = None
     m = coef_ref.shape[2] // 6
+    flat = coef_ref[:, 0, :]
+    columns = [flat[:, j * m:(j + 1) * m] for j in range(6)]
     for d in range(count):
-        row = coef_ref[d]
-        a0, b0, c0 = row[:, 0:m], row[:, m:2 * m], row[:, 2 * m:3 * m]
-        a1, b1, c1 = row[:, 3 * m:4 * m], row[:, 4 * m:5 * m], row[:, 5 * m:6 * m]
+        a0, b0, c0, a1, b1, c1 = (column[d:d + 1] for column in columns)
         if d == 0:
             g, h = a0, c0
             p, q = a1, c1

time: 150 us -> 150 us (level)
  no operation moved by 1% of the time
where the time goes in v7:
time: 150 us; the launch traced here: 149 us
  blocking collectives  80.1 us (53%)
  Pallas kernels  30.8 us (21%)
  waiting for transfers between devices  25.7 us (17%)
  local copies, waits for them, and re-layouts  6.02 us (4%)
  starting transfers between devices  4.74 us (3%)
    all_to_all x2, blocking collectives, solve_along_0(): gathered = lax.all_to_all(coef, axis, 0, 0, tiled=True)  69.4 us
    pallas_call x2, Pallas kernels, reduced_solve(): pl.pallas_call(reduced_kernel, out_shape=jax.ShapeDtypeStruct((count, 2,...  27.4 us
    all_to_all x1, waiting for transfers between devices, solve_along_0(): ends = lax.all_to_all(ends, axis, 0, 0, tiled=True)  25.7 us
    all_to_all x1, blocking collectives, solve_along_0(): ends = lax.all_to_all(ends, axis, 0, 0, tiled=True)  10.8 us
    all_to_all x1, starting transfers between devices, solve_along_0(): ends = lax.all_to_all(ends, axis, 0, 0, tiled=True)  4.74 us
    pallas_call x2, Pallas kernels, local_solve(): pl.pallas_call(local_kernel, out_shape=(shape, shape, shape, ends))(f, k, r)  3.43 us
  transfers between devices with their start and end apart: 1, of which 1 were waited for; matrix products, arithmetic and copies ran while one was open for 0% of the time, Pallas kernels for 0%

profile of v7, /device:TPU:2, one launch (start us, length us, event | category | flops | bytes accessed | tf_op | source)
XLA Modules:
  0.0 148.8 jit_solution(13545498161493447872)
XLA Ops:
  0.0 1.7 %shard_map.46 = (f32[8,16,128]{2,1,0:T(8,128)}, f32[8,16,128]{2,1,0:T(8,128)}, f32[8,16,128]{2,1,0:T(8,128)}, f32[6,16,128]{2,1,0:T(8,128)}) custom-call(f32[8,16,128]{2,1,0:T(8,128)} %f_ref.1, f32[8,16,128]{2,1,0:T(8,128)} %k_ref.1, f32[8,16,128]{2,1,0:T(8,128)} %r_ref.1), custom_call_target="tpu_custom_call" | custom-call | tf_op jit(solution)/shard_map/pallas_call | solution.py:40
  1.7 0.9 reshape.22
  2.6 0.1 copy.13
  2.7 0.1 copy.14
  2.8 55.6 %all_to_all.20.coef_ref = f32[64,1,192]{2,1,0:T(1,128)} all-to-all(f32[64,1,192]{2,1,0:T(1,128)S(1)} %copy.14), channel_id=1, replica_groups=mesh['gx'=64,'gy'=16] {'gx'}, dimensions={0} | all-to-all | bytes 98304 | tf_op jit(solution)/shard_map/all_to_all | solution.py:93
  58.4 23.8 %shard_map.47 = f32[64,2,32]{2,1,0:T(2,128)} custom-call(f32[64,1,192]{2,1,0:T(1,128)} %all_to_all.20.coef_ref), custom_call_target="tpu_custom_call" | custom-call | tf_op jit(solution)/shard_map/pallas_call | solution.py:80
  82.2 0.0 copy-start
  82.2 0.0 copy-start.4
  82.2 4.7 %all-to-all-start.1 = ((f32[64,2,32]{2,1,0:T(2,128)}), f32[64,2,32]{2,1,0:T(2,128)S(1)}, u32[]{:S(2)}, u32[]{:S(2)}) async-start(f32[64,2,32]{2,1,0:T(2,128)} %shard_map.47), calls=%async_computation.1 | async-start | bytes 131072 | tf_op jit(solution)/shard_map/all_to_all | solution.py:95
  87.0 0.0 copy-done
  87.0 0.0 copy-done.4
  87.0 0.7 copy_bitcast_fusion.1
  87.7 25.7 %all-to-all-done.1 = f32[64,2,32]{2,1,0:T(2,128)S(1)} async-done(((f32[64,2,32]{2,1,0:T(2,128)}), f32[64,2,32]{2,1,0:T(2,128)S(1)}, u32[]{:S(2)}, u32[]{:S(2)}) %all-to-all-start.1) | async-done | bytes 16416 | tf_op jit(solution)/shard_map/all_to_all | solution.py:95
  113.3 0.0 copy-start.2
  113.3 0.0 copy-start.3
  113.3 0.2 slice_reduce_fusion.1
  113.5 0.0 copy-start.1
  113.5 0.1 mul.43
  113.6 0.1 mul.40
  113.7 0.5 copy-done.2
  114.2 0.0 copy-done.3
  114.2 0.2 copy-done.1
  114.4 0.7 fusion.1.f_ref
  115.1 1.8 %shard_map.48 = (f32[16,8,128]{2,1,0:T(8,128)}, f32[16,8,128]{2,1,0:T(8,128)}, f32[16,8,128]{2,1,0:T(8,128)}, f32[6,8,128]{2,1,0:T(8,128)}) custom-call(f32[16,8,128]{2,1,0:T(8,128)} %fusion.1.f_ref, f32[16,8,128]{2,1,0:T(8,128)} %get-tuple-element.26.k_ref, f32[16,8,128]{2,1,0:T(8,128)} %get-tuple-element.25.r_ref), custom_call_target="tpu_custom_call" | custom-call | tf_op jit(solution)/shard_map/pallas_call | solution.py:40
  116.8 0.8 reshape.24
  117.7 0.1 reshape.26
  117.8 0.0 copy-start.7
  117.8 13.7 %all_to_all.21.coef_ref = f32[16,1,384]{2,1,0:T(1,128)} all-to-all(f32[16,1,384]{2,1,0:T(1,128)S(1)} %reshape.26), channel_id=1, replica_groups=mesh['gx'=64,'gy'=16] {'gy'}, dimensions={0} | all-to-all | bytes 49152 | tf_op jit(solution)/shard_map/all_to_all | solution.py:93
  131.5 3.6 %shard_map.49 = f32[16,2,64]{2,1,0:T(2,128)} custom-call(f32[16,1,384]{2,1,0:T(1,128)} %all_to_all.21.coef_ref), custom_call_target="tpu_custom_call" | custom-call | tf_op jit(solution)/shard_map/pallas_call | solution.py:80
  135.1 0.0 copy-start.6
  135.1 0.8 reshape.49
  135.9 0.0 copy-start.5
  135.9 10.8 %all_to_all.22 = f32[16,1,128]{2,1,0:T(1,128)S(1)} all-to-all(f32[16,1,128]{2,1,0:T(1,128)S(1)} %reshape.49), channel_id=1, replica_groups=mesh['gx'=64,'gy'=16] {'gy'}, dimensions={0} | all-to-all | bytes 16384 | tf_op jit(solution)/shard_map/all_to_all | solution.py:95
  146.7 0.5 broadcast.12
  147.2 0.7 reduce.16
  147.9 0.1 reshape.50
  148.0 0.1 mul.49
  148.1 0.1 mul.46
  148.1 0.0 copy-done.7
  148.1 0.0 copy-done.6
  148.1 0.0 copy-done.5
  148.2 0.6 copy.22
  (3 shorter events, 0.1 us)
Async XLA Ops:
  82.2 4.8 %copy-start = (f32[8,16,128]{2,1,0:T(8,128)S(1)}, f32[8,16,128]{2,1,0:T(8,128)}, u32[]{:S(2)}) copy-start(f32[8,16,128]{2,1,0:T(8,128)} %r_ref.1) | copy-start | bytes 196612
  82.2 4.8 %copy-start.4 = (f32[8,16,128]{2,1,0:T(8,128)S(1)}, f32[8,16,128]{2,1,0:T(8,128)}, u32[]{:S(2)}) copy-start(f32[8,16,128]{2,1,0:T(8,128)} %param.6) | copy-start | bytes 196612
  82.2 31.1 %all-to-all-start.1 = ((f32[64,2,32]{2,1,0:T(2,128)}), f32[64,2,32]{2,1,0:T(2,128)S(1)}, u32[]{:S(2)}, u32[]{:S(2)}) async-start(f32[64,2,32]{2,1,0:T(2,128)} %shard_map.47), calls=%async_computation.1 | async-start | bytes 131072 | tf_op jit(solution)/shard_map/all_to_all | solution.py:95
  113.3 0.8 copy-start.2
  113.3 0.9 copy-start.3
  113.5 0.9 copy-start.1
  117.8 30.4 %copy-start.7 = (f32[16,8,128]{2,1,0:T(8,128)S(1)}, f32[16,8,128]{2,1,0:T(8,128)}, u32[]{:S(2)}) copy-start(f32[16,8,128]{2,1,0:T(8,128)} %get-tuple-element.20) | copy-start | bytes 196612
  135.1 13.1 %copy-start.6 = (f32[16,8,128]{2,1,0:T(8,128)S(1)}, f32[16,8,128]{2,1,0:T(8,128)}, u32[]{:S(2)}) copy-start(f32[16,8,128]{2,1,0:T(8,128)} %get-tuple-element.18) | copy-start | bytes 196612
  135.9 12.2 %copy-start.5 = (f32[16,8,128]{2,1,0:T(8,128)S(1)}, f32[16,8,128]{2,1,0:T(8,128)}, u32[]{:S(2)}) copy-start(f32[16,8,128]{2,1,0:T(8,128)} %get-tuple-element.17) | copy-start | bytes 196612

commit v8 on v5

--- a/solution.py
+++ b/solution.py
@@ -11,16 +11,16 @@
     ratio, shifted, shifted_b = zero, zero, zero
     for i in range(n):
         link = k_ref[i]
-        denom = r_ref[i] + 2.0 * link + link * ratio
-        ratio = -link / denom
-        shifted = (f_ref[i] + link * shifted) / denom
-        shifted_b = (link if i == 0 else link * shifted_b) / denom
+        inverse = 1.0 / (r_ref[i] + 2.0 * link + link * ratio)
+        ratio = -link * inverse
+        shifted = (f_ref[i] + link * shifted) * inverse
+        shifted_b = (link if i == 0 else link * shifted_b) * inverse
         a_ref[i] = shifted
         b_ref[i] = shifted_b
         c_ref[i] = ratio
     later_a = a_ref[n - 1]
     later_b = b_ref[n - 1]
-    later_c = k_ref[n - 1] / denom
+    later_c = k_ref[n - 1] * inverse
     c_ref[n - 1] = later_c
     for i in range(n - 2, -1, -1):
         ratio = c_ref[i]
@@ -53,9 +53,9 @@
             g, h = a0, c0
             p, q = a1, c1
         else:
-            denom = 1.0 - b0 * q_prev
-            g = (a0 + b0 * p_prev) / denom
-            h = c0 / denom
+            inverse = 1.0 / (1.0 - b0 * q_prev)
+            g = (a0 + b0 * p_prev) * inverse
+            h = c0 * inverse
             p = a1 + b1 * p_prev + b1 * q_prev * g
             q = c1 + b1 * q_prev * h
         gains.append((g, h, p, q))

time: 130 us -> 130 us (level)
  no operation moved by 1% of the time
where the time goes in v8:
time: 130 us; the launch traced here: 129 us
  blocking collectives  79.8 us (61%)
  waiting for transfers between devices  25.7 us (20%)
  Pallas kernels  8 us (6%)
  local copies, waits for them, and re-layouts  7.65 us (6%)
  starting transfers between devices  4.73 us (4%)
  other arithmetic  2.96 us (2%)
    all_to_all x2, blocking collectives, solve_along_0(): gathered = lax.all_to_all(coef, axis, 0, 0, tiled=True)  69 us
    all_to_all x1, waiting for transfers between devices, solve_along_0(): ends = lax.all_to_all(ends, axis, 0, 0, tiled=True)  25.7 us
    all_to_all x1, blocking collectives, solve_along_0(): ends = lax.all_to_all(ends, axis, 0, 0, tiled=True)  10.8 us
    all_to_all x1, starting transfers between devices, solve_along_0(): ends = lax.all_to_all(ends, axis, 0, 0, tiled=True)  4.73 us
    pallas_call x2, Pallas kernels, reduced_solve(): pl.pallas_call(reduced_kernel, out_shape=jax.ShapeDtypeStruct((count, 2,...  4.55 us
    pallas_call x2, Pallas kernels, local_solve(): pl.pallas_call(local_kernel, out_shape=(shape, shape, shape, ends))(f, k, r)  3.45 us
    unnamed x22, local copies, waits for them, and re-layouts  3.4 us
  transfers between devices with their start and end apart: 1, of which 1 were waited for; matrix products, arithmetic and copies ran while one was open for 1% of the time, Pallas kernels for 0%

profile of v8, /device:TPU:2, one launch (start us, length us, event | category | flops | bytes accessed | tf_op | source)
XLA Modules:
  0.0 128.9 jit_solution(2513778053463617712)
XLA Ops:
  0.0 1.7 %shard_map.46 = (f32[8,16,128]{2,1,0:T(8,128)}, f32[8,16,128]{2,1,0:T(8,128)}, f32[8,16,128]{2,1,0:T(8,128)}, f32[6,16,128]{2,1,0:T(8,128)}) custom-call(f32[8,16,128]{2,1,0:T(8,128)} %f_ref.1, f32[8,16,128]{2,1,0:T(8,128)} %k_ref.1, f32[8,16,128]{2,1,0:T(8,128)} %r_ref.1), custom_call_target="tpu_custom_call" | custom-call | tf_op jit(solution)/shard_map/pallas_call | solution.py:40
  1.7 0.9 reshape.16
  2.6 0.1 copy.34
  2.7 0.2 reshape.40
  2.9 55.5 %all_to_all.20 = f32[64,1,192]{2,1,0:T(1,128)S(1)} all-to-all(f32[64,1,192]{2,1,0:T(1,128)S(1)} %reshape.40), channel_id=1, replica_groups=mesh['gx'=64,'gy'=16] {'gx'}, dimensions={0} | all-to-all | bytes 98304 | tf_op jit(solution)/shard_map/all_to_all | solution.py:92
  58.4 0.6 broadcast.12
  59.0 0.8 reduce.16
  59.8 0.8 reshape.41.coef_ref
  60.6 2.8 %shard_map.47 = f32[64,2,32]{2,1,0:T(2,128)} custom-call(f32[64,6,32]{2,1,0:T(8,128)} %reshape.41.coef_ref), custom_call_target="tpu_custom_call" | custom-call | tf_op jit(solution)/shard_map/pallas_call | solution.py:79
  63.4 0.0 copy-start
  63.4 0.0 copy-start.4
  63.4 4.7 %all-to-all-start.1 = ((f32[64,2,32]{2,1,0:T(2,128)}), f32[64,2,32]{2,1,0:T(2,128)S(1)}, u32[]{:S(2)}, u32[]{:S(2)}) async-start(f32[64,2,32]{2,1,0:T(2,128)} %shard_map.47), calls=%async_computation.1 | async-start | bytes 131072 | tf_op jit(solution)/shard_map/all_to_all | solution.py:94
  68.1 0.0 copy-done
  68.1 0.0 copy-done.4
  68.1 0.7 copy_bitcast_fusion.2
  68.8 25.7 %all-to-all-done.1 = f32[64,2,32]{2,1,0:T(2,128)S(1)} async-done(((f32[64,2,32]{2,1,0:T(2,128)}), f32[64,2,32]{2,1,0:T(2,128)S(1)}, u32[]{:S(2)}, u32[]{:S(2)}) %all-to-all-start.1) | async-done | bytes 16416 | tf_op jit(solution)/shard_map/all_to_all | solution.py:94
  94.5 0.0 copy-start.2
  94.5 0.0 copy-start.3
  94.5 0.2 slice_reduce_fusion.1
  94.7 0.0 copy-start.1
  94.7 0.1 mul.43
  94.8 0.1 mul.40
  94.8 0.5 copy-done.2
  95.3 0.0 copy-done.3
  95.4 0.2 copy-done.1
  95.6 0.7 fusion.1.f_ref
  96.2 1.8 %shard_map.48 = (f32[16,8,128]{2,1,0:T(8,128)}, f32[16,8,128]{2,1,0:T(8,128)}, f32[16,8,128]{2,1,0:T(8,128)}, f32[6,8,128]{2,1,0:T(8,128)}) custom-call(f32[16,8,128]{2,1,0:T(8,128)} %fusion.1.f_ref, f32[16,8,128]{2,1,0:T(8,128)} %get-tuple-element.26.k_ref, f32[16,8,128]{2,1,0:T(8,128)} %get-tuple-element.25.r_ref), custom_call_target="tpu_custom_call" | custom-call | tf_op jit(solution)/shard_map/pallas_call | solution.py:40
  98.0 0.8 reshape.17
  98.9 0.1 reshape.42
  99.0 13.5 %all_to_all.21 = f32[16,1,384]{2,1,0:T(1,128)S(1)} all-to-all(f32[16,1,384]{2,1,0:T(1,128)S(1)} %reshape.42), channel_id=1, replica_groups=mesh['gx'=64,'gy'=16] {'gy'}, dimensions={0} | all-to-all | bytes 49152 | tf_op jit(solution)/shard_map/all_to_all | solution.py:92
  112.5 0.7 reduce.17
  113.2 0.7 reshape.43.coef_ref
  113.9 0.0 copy-start.7
  113.9 1.8 %shard_map.49 = f32[16,2,64]{2,1,0:T(2,128)} custom-call(f32[16,6,64]{2,1,0:T(8,128)} %reshape.43.coef_ref), custom_call_target="tpu_custom_call" | custom-call | tf_op jit(solution)/shard_map/pallas_call | solution.py:79
  115.7 0.0 copy-start.6
  115.7 0.8 reshape.44
  116.5 0.0 copy-start.5
  116.5 10.8 %all_to_all.22 = f32[16,1,128]{2,1,0:T(1,128)S(1)} all-to-all(f32[16,1,128]{2,1,0:T(1,128)S(1)} %reshape.44), channel_id=1, replica_groups=mesh['gx'=64,'gy'=16] {'gy'}, dimensions={0} | all-to-all | bytes 16384 | tf_op jit(solution)/shard_map/all_to_all | solution.py:94
  127.3 0.7 reduce.18
  128.0 0.1 reshape.45
  128.1 0.1 mul.49
  128.2 0.1 mul.46
  128.2 0.0 copy-done.7
  128.2 0.0 copy-done.6
  128.2 0.0 copy-done.5
  128.3 0.6 copy.18
  (3 shorter events, 0.1 us)
Async XLA Ops:
  63.4 4.7 %copy-start = (f32[8,16,128]{2,1,0:T(8,128)S(1)}, f32[8,16,128]{2,1,0:T(8,128)}, u32[]{:S(2)}) copy-start(f32[8,16,128]{2,1,0:T(8,128)} %r_ref.1) | copy-start | bytes 196612
  63.4 4.8 %copy-start.4 = (f32[8,16,128]{2,1,0:T(8,128)S(1)}, f32[8,16,128]{2,1,0:T(8,128)}, u32[]{:S(2)}) copy-start(f32[8,16,128]{2,1,0:T(8,128)} %param.6) | copy-start | bytes 196612
  63.4 31.1 %all-to-all-start.1 = ((f32[64,2,32]{2,1,0:T(2,128)}), f32[64,2,32]{2,1,0:T(2,128)S(1)}, u32[]{:S(2)}, u32[]{:S(2)}) async-start(f32[64,2,32]{2,1,0:T(2,128)} %shard_map.47), calls=%async_computation.1 | async-start | bytes 131072 | tf_op jit(solution)/shard_map/all_to_all | solution.py:94
  94.5 0.8 copy-start.2
  94.5 0.9 copy-start.3
  94.7 0.9 copy-start.1
  113.9 14.3 %copy-start.7 = (f32[16,8,128]{2,1,0:T(8,128)S(1)}, f32[16,8,128]{2,1,0:T(8,128)}, u32[]{:S(2)}) copy-start(f32[16,8,128]{2,1,0:T(8,128)} %get-tuple-element.20) | copy-start | bytes 196612
  115.7 12.6 %copy-start.6 = (f32[16,8,128]{2,1,0:T(8,128)S(1)}, f32[16,8,128]{2,1,0:T(8,128)}, u32[]{:S(2)}) copy-start(f32[16,8,128]{2,1,0:T(8,128)} %get-tuple-element.18) | copy-start | bytes 196612
  116.5 11.7 %copy-start.5 = (f32[16,8,128]{2,1,0:T(8,128)S(1)}, f32[16,8,128]{2,1,0:T(8,128)}, u32[]{:S(2)}) copy-start(f32[16,8,128]{2,1,0:T(8,128)} %get-tuple-element.17) | copy-start | bytes 196612

commit v9 on v5

--- a/solution.py
+++ b/solution.py
@@ -42,36 +42,69 @@
 
 def reduced_kernel(coef_ref, out_ref):
     count = coef_ref.shape[0]
-    gains = []
-    p_prev = None
-    q_prev = None
-    for d in range(count):
-        row = coef_ref[d]
-        a0, b0, c0 = row[0:1], row[1:2], row[2:3]
-        a1, b1, c1 = row[3:4], row[4:5], row[5:6]
+    rows = [coef_ref[d] for d in range(count)]
+    parts = [tuple(row[j:j + 1] for j in range(6)) for row in rows]
+    zero = jnp.zeros_like(parts[0][0])
+    mid = count // 2
+    left = []
+    p_prev = q_prev = None
+    for d in range(mid):
+        a0, b0, c0, a1, b1, c1 = parts[d]
         if d == 0:
-            g, h = a0, c0
-            p, q = a1, c1
+            g, h, p, q = a0, c0, a1, c1
         else:
             denom = 1.0 - b0 * q_prev
             g = (a0 + b0 * p_prev) / denom
             h = c0 / denom
             p = a1 + b1 * p_prev + b1 * q_prev * g
             q = c1 + b1 * q_prev * h
-        gains.append((g, h, p, q))
+        left.append((g, h, p, q))
         p_prev, q_prev = p, q
-    later = jnp.zeros_like(gains[0][0])
-    for d in range(count - 1, -1, -1):
-        g, h, _, _ = gains[d]
+    right = [None] * count
+    u_next = v_next = None
+    for d in range(count - 1, mid - 1, -1):
+        a0, b0, c0, a1, b1, c1 = parts[d]
+        if d == count - 1:
+            s_d, t_d, u, v = a1, b1, a0, b0
+        else:
+            denom = 1.0 - c1 * v_next
+            s_d = (a1 + c1 * u_next) / denom
+            t_d = b1 / denom
+            u = a0 + c0 * u_next + c0 * v_next * s_d
+            v = b0 + c0 * v_next * t_d
+        right[d] = (s_d, t_d, u, v)
+        u_next, v_next = u, v
+    if mid == 0:
+        out_ref[0, 0:1, :] = zero
+        out_ref[0, 1:2, :] = zero
+        return
+    p, q = left[mid - 1][2], left[mid - 1][3]
+    u, v = right[mid][2], right[mid][3]
+    meet_last = (p + q * u) / (1.0 - q * v)
+    meet_first = u + v * meet_last
+    later = meet_first
+    for d in range(mid - 1, -1, -1):
+        g, h, _, _ = left[d]
         first = g + h * later
         if d > 0:
-            _, _, p, q = gains[d - 1]
+            _, _, p, q = left[d - 1]
             before = p + q * first
         else:
-            before = jnp.zeros_like(first)
+            before = zero
         out_ref[d, 0:1, :] = before
         out_ref[d, 1:2, :] = later
         later = first
+    last = meet_last
+    for d in range(mid, count):
+        s_d, t_d, _, _ = right[d]
+        out_ref[d, 0:1, :] = last
+        last = s_d + t_d * last
+        if d + 1 < count:
+            _, _, u, v = right[d + 1]
+            after = u + v * last
+        else:
+            after = zero
+        out_ref[d, 1:2, :] = after
 
 
 def reduced_solve(coef):

time: 130 us -> 129 us (level)
  no operation moved by 1% of the time
where the time goes in v9:
time: 129 us; the launch traced here: 128 us
  blocking collectives  79.8 us (62%)
  waiting for transfers between devices  25.7 us (20%)
  local copies, waits for them, and re-layouts  7.65 us (6%)
  Pallas kernels  7.28 us (6%)
  starting transfers between devices  4.73 us (4%)
  other arithmetic  2.96 us (2%)
    all_to_all x2, blocking collectives, solve_along_0(): gathered = lax.all_to_all(coef, axis, 0, 0, tiled=True)  69 us
    all_to_all x1, waiting for transfers between devices, solve_along_0(): ends = lax.all_to_all(ends, axis, 0, 0, tiled=True)  25.7 us
    all_to_all x1, blocking collectives, solve_along_0(): ends = lax.all_to_all(ends, axis, 0, 0, tiled=True)  10.8 us
    all_to_all x1, starting transfers between devices, solve_along_0(): ends = lax.all_to_all(ends, axis, 0, 0, tiled=True)  4.73 us
    pallas_call x2, Pallas kernels, reduced_solve(): pl.pallas_call(reduced_kernel, out_shape=jax.ShapeDtypeStruct((count, 2,...  3.83 us
    pallas_call x2, Pallas kernels, local_solve(): pl.pallas_call(local_kernel, out_shape=(shape, shape, shape, ends))(f, k, r)  3.45 us
    unnamed x22, local copies, waits for them, and re-layouts  3.4 us
  transfers between devices with their start and end apart: 1, of which 1 were waited for; matrix products, arithmetic and copies ran while one was open for 1% of the time, Pallas kernels for 0%

profile of v9, /device:TPU:2, one launch (start us, length us, event | category | flops | bytes accessed | tf_op | source)
XLA Modules:
  0.0 128.2 jit_solution(4488903244216461903)
XLA Ops:
  0.0 1.7 %shard_map.46 = (f32[8,16,128]{2,1,0:T(8,128)}, f32[8,16,128]{2,1,0:T(8,128)}, f32[8,16,128]{2,1,0:T(8,128)}, f32[6,16,128]{2,1,0:T(8,128)}) custom-call(f32[8,16,128]{2,1,0:T(8,128)} %f_ref.1, f32[8,16,128]{2,1,0:T(8,128)} %k_ref.1, f32[8,16,128]{2,1,0:T(8,128)} %r_ref.1), custom_call_target="tpu_custom_call" | custom-call | tf_op jit(solution)/shard_map/pallas_call | solution.py:40
  1.7 0.9 reshape.16
  2.6 0.1 copy.34
  2.7 0.2 reshape.40
  2.9 55.5 %all_to_all.20 = f32[64,1,192]{2,1,0:T(1,128)S(1)} all-to-all(f32[64,1,192]{2,1,0:T(1,128)S(1)} %reshape.40), channel_id=1, replica_groups=mesh['gx'=64,'gy'=16] {'gx'}, dimensions={0} | all-to-all | bytes 98304 | tf_op jit(solution)/shard_map/all_to_all | solution.py:125
  58.4 0.6 broadcast.12
  59.0 0.8 reduce.16
  59.8 0.8 reshape.41.coef_ref
  60.6 2.2 %shard_map.47 = f32[64,2,32]{2,1,0:T(2,128)} custom-call(f32[64,6,32]{2,1,0:T(8,128)} %reshape.41.coef_ref), custom_call_target="tpu_custom_call" | custom-call | tf_op jit(solution)/shard_map/pallas_call | solution.py:112
  62.8 0.0 copy-start
  62.8 0.0 copy-start.4
  62.8 4.7 %all-to-all-start.1 = ((f32[64,2,32]{2,1,0:T(2,128)}), f32[64,2,32]{2,1,0:T(2,128)S(1)}, u32[]{:S(2)}, u32[]{:S(2)}) async-start(f32[64,2,32]{2,1,0:T(2,128)} %shard_map.47), calls=%async_computation.1 | async-start | bytes 131072 | tf_op jit(solution)/shard_map/all_to_all | solution.py:127
  67.5 0.0 copy-done
  67.5 0.0 copy-done.4
  67.6 0.7 copy_bitcast_fusion.2
  68.2 25.7 %all-to-all-done.1 = f32[64,2,32]{2,1,0:T(2,128)S(1)} async-done(((f32[64,2,32]{2,1,0:T(2,128)}), f32[64,2,32]{2,1,0:T(2,128)S(1)}, u32[]{:S(2)}, u32[]{:S(2)}) %all-to-all-start.1) | async-done | bytes 16416 | tf_op jit(solution)/shard_map/all_to_all | solution.py:127
  93.9 0.0 copy-start.2
  93.9 0.0 copy-start.3
  93.9 0.2 slice_reduce_fusion.1
  94.1 0.0 copy-start.1
  94.1 0.1 mul.43
  94.2 0.1 mul.40
  94.3 0.5 copy-done.2
  94.8 0.0 copy-done.3
  94.8 0.2 copy-done.1
  95.0 0.7 fusion.1.f_ref
  95.7 1.8 %shard_map.48 = (f32[16,8,128]{2,1,0:T(8,128)}, f32[16,8,128]{2,1,0:T(8,128)}, f32[16,8,128]{2,1,0:T(8,128)}, f32[6,8,128]{2,1,0:T(8,128)}) custom-call(f32[16,8,128]{2,1,0:T(8,128)} %fusion.1.f_ref, f32[16,8,128]{2,1,0:T(8,128)} %get-tuple-element.26.k_ref, f32[16,8,128]{2,1,0:T(8,128)} %get-tuple-element.25.r_ref), custom_call_target="tpu_custom_call" | custom-call | tf_op jit(solution)/shard_map/pallas_call | solution.py:40
  97.4 0.8 reshape.17
  98.3 0.1 reshape.42
  98.4 13.5 %all_to_all.21 = f32[16,1,384]{2,1,0:T(1,128)S(1)} all-to-all(f32[16,1,384]{2,1,0:T(1,128)S(1)} %reshape.42), channel_id=1, replica_groups=mesh['gx'=64,'gy'=16] {'gy'}, dimensions={0} | all-to-all | bytes 49152 | tf_op jit(solution)/shard_map/all_to_all | solution.py:125
  111.9 0.7 reduce.17
  112.6 0.7 reshape.43.coef_ref
  113.3 0.0 copy-start.7
  113.3 1.6 %shard_map.49 = f32[16,2,64]{2,1,0:T(2,128)} custom-call(f32[16,6,64]{2,1,0:T(8,128)} %reshape.43.coef_ref), custom_call_target="tpu_custom_call" | custom-call | tf_op jit(solution)/shard_map/pallas_call | solution.py:112
  114.9 0.0 copy-start.6
  114.9 0.8 reshape.44
  115.8 0.0 copy-start.5
  115.8 10.8 %all_to_all.22 = f32[16,1,128]{2,1,0:T(1,128)S(1)} all-to-all(f32[16,1,128]{2,1,0:T(1,128)S(1)} %reshape.44), channel_id=1, replica_groups=mesh['gx'=64,'gy'=16] {'gy'}, dimensions={0} | all-to-all | bytes 16384 | tf_op jit(solution)/shard_map/all_to_all | solution.py:127
  126.5 0.7 reduce.18
  127.2 0.1 reshape.45
  127.4 0.1 mul.49
  127.4 0.1 mul.46
  127.5 0.0 copy-done.7
  127.5 0.0 copy-done.6
  127.5 0.0 copy-done.5
  127.5 0.6 copy.18
  (3 shorter events, 0.1 us)
Async XLA Ops:
  62.8 4.7 %copy-start = (f32[8,16,128]{2,1,0:T(8,128)S(1)}, f32[8,16,128]{2,1,0:T(8,128)}, u32[]{:S(2)}) copy-start(f32[8,16,128]{2,1,0:T(8,128)} %r_ref.1) | copy-start | bytes 196612
  62.8 4.8 %copy-start.4 = (f32[8,16,128]{2,1,0:T(8,128)S(1)}, f32[8,16,128]{2,1,0:T(8,128)}, u32[]{:S(2)}) copy-start(f32[8,16,128]{2,1,0:T(8,128)} %param.6) | copy-start | bytes 196612
  62.8 31.1 %all-to-all-start.1 = ((f32[64,2,32]{2,1,0:T(2,128)}), f32[64,2,32]{2,1,0:T(2,128)S(1)}, u32[]{:S(2)}, u32[]{:S(2)}) async-start(f32[64,2,32]{2,1,0:T(2,128)} %shard_map.47), calls=%async_computation.1 | async-start | bytes 131072 | tf_op jit(solution)/shard_map/all_to_all | solution.py:127
  93.9 0.8 copy-start.2
  93.9 0.9 copy-start.3
  94.1 0.9 copy-start.1
  113.3 14.2 %copy-start.7 = (f32[16,8,128]{2,1,0:T(8,128)S(1)}, f32[16,8,128]{2,1,0:T(8,128)}, u32[]{:S(2)}) copy-start(f32[16,8,128]{2,1,0:T(8,128)} %get-tuple-element.20) | copy-start | bytes 196612
  114.9 12.6 %copy-start.6 = (f32[16,8,128]{2,1,0:T(8,128)S(1)}, f32[16,8,128]{2,1,0:T(8,128)}, u32[]{:S(2)}) copy-start(f32[16,8,128]{2,1,0:T(8,128)} %get-tuple-element.18) | copy-start | bytes 196612
  115.8 11.7 %copy-start.5 = (f32[16,8,128]{2,1,0:T(8,128)S(1)}, f32[16,8,128]{2,1,0:T(8,128)}, u32[]{:S(2)}) copy-start(f32[16,8,128]{2,1,0:T(8,128)} %get-tuple-element.17) | copy-start | bytes 196612

commit v10 on v9

--- a/solution.py
+++ b/solution.py
@@ -30,13 +30,31 @@
         a_ref[i] = later_a
         b_ref[i] = later_b
         c_ref[i] = later_c
-    for j, (ref, at) in enumerate(((a_ref, 0), (b_ref, 0), (c_ref, 0), (a_ref, n - 1), (b_ref, n - 1), (c_ref, n - 1))):
-        e_ref[j] = ref[at]
+    ends = ((a_ref, 0), (b_ref, 0), (c_ref, 0), (a_ref, n - 1), (b_ref, n - 1), (c_ref, n - 1))
+    if e_ref.shape[0] == 6 and len(e_ref.shape) == 3 and e_ref.shape[1:] == a_ref.shape[1:]:
+        for j, (ref, at) in enumerate(ends):
+            e_ref[j] = ref[at]
+        return
+    count, _, m = e_ref.shape
+    per_row = a_ref.shape[2] // m
+    for c, (ref, at) in enumerate(ends):
+        value = ref[at]
+        for j in range(count):
+            row, lane = j // per_row, (j % per_row) * m
+            e_ref[j, c:c + 1, :] = value[row:row + 1, lane:lane + m]
 
 
-def local_solve(f, k, r):
+def chunked(f, count):
+    m = f.shape[1] * f.shape[2] // count
+    return m <= f.shape[2] and f.shape[2] % m == 0 and count != 6
+
+
+def local_solve(f, k, r, count):
     shape = jax.ShapeDtypeStruct(f.shape, f.dtype)
-    ends = jax.ShapeDtypeStruct((6,) + f.shape[1:], f.dtype)
+    if chunked(f, count):
+        ends = jax.ShapeDtypeStruct((count, 6, f.shape[1] * f.shape[2] // count), f.dtype)
+    else:
+        ends = jax.ShapeDtypeStruct((6,) + f.shape[1:], f.dtype)
     return pl.pallas_call(local_kernel, out_shape=(shape, shape, shape, ends))(f, k, r)
 
 
@@ -117,11 +135,9 @@
 def solve_along_0(f, k, r, axis):
     count = lax.axis_size(axis)
     n, rows, lanes = f.shape
-    a, b, c, coef = local_solve(f, k, r)
-    lines = rows * lanes
-    m = lines // count
-    coef = coef.reshape(6, count, m)
-    coef = jnp.transpose(coef, (1, 0, 2))
+    a, b, c, coef = local_solve(f, k, r, count)
+    if not chunked(f, count):
+        coef = jnp.transpose(coef.reshape(6, count, rows * lanes // count), (1, 0, 2))
     gathered = lax.all_to_all(coef, axis, 0, 0, tiled=True)
     ends = reduced_solve(gathered)
     ends = lax.all_to_all(ends, axis, 0, 0, tiled=True)

time: 129 us -> 129 us (level)
    unnamed x22 -> x23, local copies, waits for them, and re-layouts: 3.4 us -> 5.82 us
    reshape x4 -> x0, local copies, waits for them, and re-layouts: 1.84 us -> none  [solve_along_0(): coef = coef.reshape(6, count, m)]
  transfers between devices with their start and end apart: 1 -> 1, of which waited for: 1 -> 1; matrix products, arithmetic and copies ran while one was open for 1% -> 0% of each run, Pallas kernels for 0% -> 0%
where the time goes in v10:
time: 129 us; the launch traced here: 128 us
  blocking collectives  79.8 us (62%)
  waiting for transfers between devices  25.7 us (20%)
  local copies, waits for them, and re-layouts  7.55 us (6%)
  Pallas kernels  7.43 us (6%)
  starting transfers between devices  4.73 us (4%)
  other arithmetic  2.98 us (2%)
    all_to_all x2, blocking collectives, solve_along_0(): gathered = lax.all_to_all(coef, axis, 0, 0, tiled=True)  69 us
    all_to_all x1, waiting for transfers between devices, solve_along_0(): ends = lax.all_to_all(ends, axis, 0, 0, tiled=True)  25.7 us
    all_to_all x1, blocking collectives, solve_along_0(): ends = lax.all_to_all(ends, axis, 0, 0, tiled=True)  10.8 us
    unnamed x23, local copies, waits for them, and re-layouts  5.82 us
    all_to_all x1, starting transfers between devices, solve_along_0(): ends = lax.all_to_all(ends, axis, 0, 0, tiled=True)  4.73 us
    pallas_call x2, Pallas kernels, reduced_solve(): pl.pallas_call(reduced_kernel, out_shape=jax.ShapeDtypeStruct((count, 2,...  3.83 us
    pallas_call x2, Pallas kernels, local_solve(): pl.pallas_call(local_kernel, out_shape=(shape, shape, shape, ends))(f, k, r)  3.6 us
  transfers between devices with their start and end apart: 1, of which 1 were waited for; matrix products, arithmetic and copies ran while one was open for 0% of the time, Pallas kernels for 0%

profile of v10, /device:TPU:2, one launch (start us, length us, event | category | flops | bytes accessed | tf_op | source)
XLA Modules:
  0.0 128.3 jit_solution(7314161661820159184)
XLA Ops:
  0.0 1.8 %shard_map.46 = (f32[8,16,128]{2,1,0:T(8,128)}, f32[8,16,128]{2,1,0:T(8,128)}, f32[8,16,128]{2,1,0:T(8,128)}, f32[64,6,32]{2,1,0:T(8,128)}) custom-call(f32[8,16,128]{2,1,0:T(8,128)} %f_ref.1, f32[8,16,128]{2,1,0:T(8,128)} %k_ref.1, f32[8,16,128]{2,1,0:T(8,128)} %r_ref.1), custom_call_target="tpu_custom_call" | custom-call | tf_op jit(solution)/shard_map/pallas_call | solution.py:58
  1.8 1.1 reshape.32
  2.9 55.5 %all_to_all.20 = f32[64,1,192]{2,1,0:T(1,128)S(1)} all-to-all(f32[64,1,192]{2,1,0:T(1,128)S(1)} %reshape.32), channel_id=1, replica_groups=mesh['gx'=64,'gy'=16] {'gx'}, dimensions={0} | all-to-all | bytes 98304 | tf_op jit(solution)/shard_map/all_to_all | solution.py:141
  58.4 0.6 broadcast.12
  59.0 0.8 reduce.16
  59.8 0.8 reshape.33.coef_ref
  60.6 2.2 %shard_map.47 = f32[64,2,32]{2,1,0:T(2,128)} custom-call(f32[64,6,32]{2,1,0:T(8,128)} %reshape.33.coef_ref), custom_call_target="tpu_custom_call" | custom-call | tf_op jit(solution)/shard_map/pallas_call | solution.py:130
  62.9 0.0 copy-start
  62.9 4.7 %all-to-all-start.1 = ((f32[64,2,32]{2,1,0:T(2,128)}), f32[64,2,32]{2,1,0:T(2,128)S(1)}, u32[]{:S(2)}, u32[]{:S(2)}) async-start(f32[64,2,32]{2,1,0:T(2,128)} %shard_map.47), calls=%async_computation.1 | async-start | bytes 131072 | tf_op jit(solution)/shard_map/all_to_all | solution.py:143
  67.6 0.0 copy-done
  67.6 0.0 copy-start.4
  67.6 0.6 copy.30
  68.3 25.7 %all-to-all-done.1 = f32[64,2,32]{2,1,0:T(2,128)S(1)} async-done(((f32[64,2,32]{2,1,0:T(2,128)}), f32[64,2,32]{2,1,0:T(2,128)S(1)}, u32[]{:S(2)}, u32[]{:S(2)}) %all-to-all-start.1) | async-done | bytes 16416 | tf_op jit(solution)/shard_map/all_to_all | solution.py:143
  94.0 0.0 copy-start.2
  94.0 0.0 copy-start.3
  94.0 0.2 slice_reduce_fusion.1
  94.2 0.0 copy-start.1
  94.2 0.1 mul.40
  94.2 0.1 mul.43
  94.3 0.0 copy-done.4
  94.3 0.5 copy-done.2
  94.8 0.0 copy-done.3
  94.8 0.2 copy-done.1
  95.0 0.7 copy_bitcast_fusion.1
  95.7 1.8 %shard_map.48 = (f32[16,8,128]{2,1,0:T(8,128)}, f32[16,8,128]{2,1,0:T(8,128)}, f32[16,8,128]{2,1,0:T(8,128)}, f32[16,6,64]{2,1,0:T(8,128)}) custom-call(f32[16,8,128]{2,1,0:T(8,128)} %get-tuple-element.26.f_ref, f32[16,8,128]{2,1,0:T(8,128)} %get-tuple-element.25.k_ref, f32[16,8,128]{2,1,0:T(8,128)} %bitcast.11), custom_call_target="tpu_custom_call" | custom-call | tf_op jit(solution)/shard_map/pallas_call | solution.py:58
  97.5 0.9 reshape.34
  98.5 13.5 %all_to_all.21 = f32[16,1,384]{2,1,0:T(1,128)S(1)} all-to-all(f32[16,1,384]{2,1,0:T(1,128)S(1)} %reshape.34), channel_id=1, replica_groups=mesh['gx'=64,'gy'=16] {'gy'}, dimensions={0} | all-to-all | bytes 49152 | tf_op jit(solution)/shard_map/all_to_all | solution.py:141
  112.0 0.7 reduce.17
  112.7 0.7 reshape.35.coef_ref
  113.4 0.0 copy-start.7
  113.4 1.6 %shard_map.49 = f32[16,2,64]{2,1,0:T(2,128)} custom-call(f32[16,6,64]{2,1,0:T(8,128)} %reshape.35.coef_ref), custom_call_target="tpu_custom_call" | custom-call | tf_op jit(solution)/shard_map/pallas_call | solution.py:130
  115.0 0.0 copy-start.6
  115.0 0.8 reshape.36
  115.9 0.0 copy-start.5
  115.9 10.8 %all_to_all.22 = f32[16,1,128]{2,1,0:T(1,128)S(1)} all-to-all(f32[16,1,128]{2,1,0:T(1,128)S(1)} %reshape.36), channel_id=1, replica_groups=mesh['gx'=64,'gy'=16] {'gy'}, dimensions={0} | all-to-all | bytes 16384 | tf_op jit(solution)/shard_map/all_to_all | solution.py:143
  126.6 0.7 reduce.18
  127.3 0.1 reshape.37
  127.5 0.1 mul.46
  127.5 0.1 mul.49
  127.6 0.0 copy-done.7
  127.6 0.0 copy-done.6
  127.6 0.0 copy-done.5
  127.6 0.6 copy.16
  (2 shorter events, 0.1 us)
Async XLA Ops:
  62.9 4.7 %copy-start = (f32[8,16,128]{2,1,0:T(8,128)S(1)}, f32[8,16,128]{2,1,0:T(8,128)}, u32[]{:S(2)}) copy-start(f32[8,16,128]{2,1,0:T(8,128)} %r_ref.1) | copy-start | bytes 196612
  62.9 31.1 %all-to-all-start.1 = ((f32[64,2,32]{2,1,0:T(2,128)}), f32[64,2,32]{2,1,0:T(2,128)S(1)}, u32[]{:S(2)}, u32[]{:S(2)}) async-start(f32[64,2,32]{2,1,0:T(2,128)} %shard_map.47), calls=%async_computation.1 | async-start | bytes 131072 | tf_op jit(solution)/shard_map/all_to_all | solution.py:143
  67.6 26.7 %copy-start.4 = (f32[8,16,128]{2,1,0:T(8,128)S(1)}, f32[8,16,128]{2,1,0:T(8,128)}, u32[]{:S(2)}) copy-start(f32[8,16,128]{2,1,0:T(8,128)} %get-tuple-element.16) | copy-start | bytes 196612
  94.0 0.8 copy-start.2
  94.0 0.9 copy-start.3
  94.2 0.9 copy-start.1
  113.4 14.2 %copy-start.7 = (f32[16,8,128]{2,1,0:T(8,128)S(1)}, f32[16,8,128]{2,1,0:T(8,128)}, u32[]{:S(2)}) copy-start(f32[16,8,128]{2,1,0:T(8,128)} %get-tuple-element.20) | copy-start | bytes 196612
  115.0 12.6 %copy-start.6 = (f32[16,8,128]{2,1,0:T(8,128)S(1)}, f32[16,8,128]{2,1,0:T(8,128)}, u32[]{:S(2)}) copy-start(f32[16,8,128]{2,1,0:T(8,128)} %get-tuple-element.18) | copy-start | bytes 196612
  115.9 11.7 %copy-start.5 = (f32[16,8,128]{2,1,0:T(8,128)S(1)}, f32[16,8,128]{2,1,0:T(8,128)}, u32[]{:S(2)}) copy-start(f32[16,8,128]{2,1,0:T(8,128)} %get-tuple-element.17) | copy-start | bytes 196612

commit v11 on v9

--- a/solution.py
+++ b/solution.py
@@ -9,29 +9,28 @@
     n = f_ref.shape[0]
     zero = jnp.zeros(f_ref.shape[1:], f_ref.dtype)
     ratio, shifted, shifted_b = zero, zero, zero
+    sweep = []
     for i in range(n):
         link = k_ref[i]
         denom = r_ref[i] + 2.0 * link + link * ratio
         ratio = -link / denom
         shifted = (f_ref[i] + link * shifted) / denom
         shifted_b = (link if i == 0 else link * shifted_b) / denom
-        a_ref[i] = shifted
-        b_ref[i] = shifted_b
-        c_ref[i] = ratio
-    later_a = a_ref[n - 1]
-    later_b = b_ref[n - 1]
+        sweep.append((ratio, shifted, shifted_b))
+    later_a, later_b = shifted, shifted_b
     later_c = k_ref[n - 1] / denom
-    c_ref[n - 1] = later_c
+    solved = [None] * n
+    solved[n - 1] = (later_a, later_b, later_c)
     for i in range(n - 2, -1, -1):
-        ratio = c_ref[i]
-        later_a = a_ref[i] - ratio * later_a
-        later_b = b_ref[i] - ratio * later_b
+        ratio, shifted, shifted_b = sweep[i]
+        later_a = shifted - ratio * later_a
+        later_b = shifted_b - ratio * later_b
         later_c = -ratio * later_c
-        a_ref[i] = later_a
-        b_ref[i] = later_b
-        c_ref[i] = later_c
-    for j, (ref, at) in enumerate(((a_ref, 0), (b_ref, 0), (c_ref, 0), (a_ref, n - 1), (b_ref, n - 1), (c_ref, n - 1))):
-        e_ref[j] = ref[at]
+        solved[i] = (later_a, later_b, later_c)
+    for i in range(n):
+        a_ref[i], b_ref[i], c_ref[i] = solved[i]
+    for j, value in enumerate(solved[0] + solved[n - 1]):
+        e_ref[j] = value
 
 
 def local_solve(f, k, r):

time: 129 us -> 129 us (level)
  no operation moved by 1% of the time
where the time goes in v11:
time: 129 us; the launch traced here: 128 us
  blocking collectives  79.8 us (62%)
  waiting for transfers between devices  25.7 us (20%)
  local copies, waits for them, and re-layouts  7.65 us (6%)
  Pallas kernels  7.28 us (6%)
  starting transfers between devices  4.73 us (4%)
  other arithmetic  2.96 us (2%)
    all_to_all x2, blocking collectives, solve_along_0(): gathered = lax.all_to_all(coef, axis, 0, 0, tiled=True)  69 us
    all_to_all x1, waiting for transfers between devices, solve_along_0(): ends = lax.all_to_all(ends, axis, 0, 0, tiled=True)  25.7 us
    all_to_all x1, blocking collectives, solve_along_0(): ends = lax.all_to_all(ends, axis, 0, 0, tiled=True)  10.8 us
    all_to_all x1, starting transfers between devices, solve_along_0(): ends = lax.all_to_all(ends, axis, 0, 0, tiled=True)  4.73 us
    pallas_call x2, Pallas kernels, reduced_solve(): pl.pallas_call(reduced_kernel, out_shape=jax.ShapeDtypeStruct((count, 2,...  3.83 us
    pallas_call x2, Pallas kernels, local_solve(): pl.pallas_call(local_kernel, out_shape=(shape, shape, shape, ends))(f, k, r)  3.45 us
    unnamed x22, local copies, waits for them, and re-layouts  3.4 us
  transfers between devices with their start and end apart: 1, of which 1 were waited for; matrix products, arithmetic and copies ran while one was open for 1% of the time, Pallas kernels for 0%

profile of v11, /device:TPU:2, one launch (start us, length us, event | category | flops | bytes accessed | tf_op | source)
XLA Modules:
  0.0 128.2 jit_solution(10714122022455353694)
XLA Ops:
  0.0 1.7 %shard_map.46 = (f32[8,16,128]{2,1,0:T(8,128)}, f32[8,16,128]{2,1,0:T(8,128)}, f32[8,16,128]{2,1,0:T(8,128)}, f32[6,16,128]{2,1,0:T(8,128)}) custom-call(f32[8,16,128]{2,1,0:T(8,128)} %f_ref.1, f32[8,16,128]{2,1,0:T(8,128)} %k_ref.1, f32[8,16,128]{2,1,0:T(8,128)} %r_ref.1), custom_call_target="tpu_custom_call" | custom-call | tf_op jit(solution)/shard_map/pallas_call | solution.py:39
  1.7 0.9 reshape.16
  2.6 0.1 copy.34
  2.7 0.2 reshape.40
  2.9 55.5 %all_to_all.20 = f32[64,1,192]{2,1,0:T(1,128)S(1)} all-to-all(f32[64,1,192]{2,1,0:T(1,128)S(1)} %reshape.40), channel_id=1, replica_groups=mesh['gx'=64,'gy'=16] {'gx'}, dimensions={0} | all-to-all | bytes 98304 | tf_op jit(solution)/shard_map/all_to_all | solution.py:124
  58.4 0.6 broadcast.12
  59.0 0.8 reduce.16
  59.8 0.8 reshape.41.coef_ref
  60.6 2.2 %shard_map.47 = f32[64,2,32]{2,1,0:T(2,128)} custom-call(f32[64,6,32]{2,1,0:T(8,128)} %reshape.41.coef_ref), custom_call_target="tpu_custom_call" | custom-call | tf_op jit(solution)/shard_map/pallas_call | solution.py:111
  62.8 0.0 copy-start
  62.8 0.0 copy-start.4
  62.8 4.7 %all-to-all-start.1 = ((f32[64,2,32]{2,1,0:T(2,128)}), f32[64,2,32]{2,1,0:T(2,128)S(1)}, u32[]{:S(2)}, u32[]{:S(2)}) async-start(f32[64,2,32]{2,1,0:T(2,128)} %shard_map.47), calls=%async_computation.1 | async-start | bytes 131072 | tf_op jit(solution)/shard_map/all_to_all | solution.py:126
  67.5 0.0 copy-done
  67.5 0.0 copy-done.4
  67.6 0.7 copy_bitcast_fusion.2
  68.2 25.7 %all-to-all-done.1 = f32[64,2,32]{2,1,0:T(2,128)S(1)} async-done(((f32[64,2,32]{2,1,0:T(2,128)}), f32[64,2,32]{2,1,0:T(2,128)S(1)}, u32[]{:S(2)}, u32[]{:S(2)}) %all-to-all-start.1) | async-done | bytes 16416 | tf_op jit(solution)/shard_map/all_to_all | solution.py:126
  93.9 0.0 copy-start.2
  93.9 0.0 copy-start.3
  93.9 0.2 slice_reduce_fusion.1
  94.1 0.0 copy-start.1
  94.1 0.1 mul.43
  94.2 0.1 mul.40
  94.3 0.5 copy-done.2
  94.8 0.0 copy-done.3
  94.8 0.2 copy-done.1
  95.0 0.7 fusion.1.f_ref
  95.7 1.8 %shard_map.48 = (f32[16,8,128]{2,1,0:T(8,128)}, f32[16,8,128]{2,1,0:T(8,128)}, f32[16,8,128]{2,1,0:T(8,128)}, f32[6,8,128]{2,1,0:T(8,128)}) custom-call(f32[16,8,128]{2,1,0:T(8,128)} %fusion.1.f_ref, f32[16,8,128]{2,1,0:T(8,128)} %get-tuple-element.26.k_ref, f32[16,8,128]{2,1,0:T(8,128)} %get-tuple-element.25.r_ref), custom_call_target="tpu_custom_call" | custom-call | tf_op jit(solution)/shard_map/pallas_call | solution.py:39
  97.4 0.8 reshape.17
  98.3 0.1 reshape.42
  98.4 13.5 %all_to_all.21 = f32[16,1,384]{2,1,0:T(1,128)S(1)} all-to-all(f32[16,1,384]{2,1,0:T(1,128)S(1)} %reshape.42), channel_id=1, replica_groups=mesh['gx'=64,'gy'=16] {'gy'}, dimensions={0} | all-to-all | bytes 49152 | tf_op jit(solution)/shard_map/all_to_all | solution.py:124
  111.9 0.7 reduce.17
  112.6 0.7 reshape.43.coef_ref
  113.3 0.0 copy-start.7
  113.3 1.6 %shard_map.49 = f32[16,2,64]{2,1,0:T(2,128)} custom-call(f32[16,6,64]{2,1,0:T(8,128)} %reshape.43.coef_ref), custom_call_target="tpu_custom_call" | custom-call | tf_op jit(solution)/shard_map/pallas_call | solution.py:111
  114.9 0.0 copy-start.6
  114.9 0.8 reshape.44
  115.8 0.0 copy-start.5
  115.8 10.8 %all_to_all.22 = f32[16,1,128]{2,1,0:T(1,128)S(1)} all-to-all(f32[16,1,128]{2,1,0:T(1,128)S(1)} %reshape.44), channel_id=1, replica_groups=mesh['gx'=64,'gy'=16] {'gy'}, dimensions={0} | all-to-all | bytes 16384 | tf_op jit(solution)/shard_map/all_to_all | solution.py:126
  126.5 0.7 reduce.18
  127.2 0.1 reshape.45
  127.4 0.1 mul.49
  127.4 0.1 mul.46
  127.5 0.0 copy-done.7
  127.5 0.0 copy-done.6
  127.5 0.0 copy-done.5
  127.5 0.6 copy.18
  (3 shorter events, 0.1 us)
Async XLA Ops:
  62.8 4.7 %copy-start = (f32[8,16,128]{2,1,0:T(8,128)S(1)}, f32[8,16,128]{2,1,0:T(8,128)}, u32[]{:S(2)}) copy-start(f32[8,16,128]{2,1,0:T(8,128)} %r_ref.1) | copy-start | bytes 196612
  62.8 4.8 %copy-start.4 = (f32[8,16,128]{2,1,0:T(8,128)S(1)}, f32[8,16,128]{2,1,0:T(8,128)}, u32[]{:S(2)}) copy-start(f32[8,16,128]{2,1,0:T(8,128)} %param.6) | copy-start | bytes 196612
  62.8 31.1 %all-to-all-start.1 = ((f32[64,2,32]{2,1,0:T(2,128)}), f32[64,2,32]{2,1,0:T(2,128)S(1)}, u32[]{:S(2)}, u32[]{:S(2)}) async-start(f32[64,2,32]{2,1,0:T(2,128)} %shard_map.47), calls=%async_computation.1 | async-start | bytes 131072 | tf_op jit(solution)/shard_map/all_to_all | solution.py:126
  93.9 0.8 copy-start.2
  93.9 0.9 copy-start.3
  94.1 0.9 copy-start.1
  113.3 14.2 %copy-start.7 = (f32[16,8,128]{2,1,0:T(8,128)S(1)}, f32[16,8,128]{2,1,0:T(8,128)}, u32[]{:S(2)}) copy-start(f32[16,8,128]{2,1,0:T(8,128)} %get-tuple-element.20) | copy-start | bytes 196612
  114.9 12.6 %copy-start.6 = (f32[16,8,128]{2,1,0:T(8,128)S(1)}, f32[16,8,128]{2,1,0:T(8,128)}, u32[]{:S(2)}) copy-start(f32[16,8,128]{2,1,0:T(8,128)} %get-tuple-element.18) | copy-start | bytes 196612
  115.8 11.7 %copy-start.5 = (f32[16,8,128]{2,1,0:T(8,128)S(1)}, f32[16,8,128]{2,1,0:T(8,128)}, u32[]{:S(2)}) copy-start(f32[16,8,128]{2,1,0:T(8,128)} %get-tuple-element.17) | copy-start | bytes 196612
